TPU v7x, 1024 devices: a whole 4x4x32 slice. The times are simulated.
1024 devices in a mesh: ctx: 128 (over z, y_lo, core), tp: 8 (over y_hi, x).
Axes of the slice: x: 4, y: 4 (y_hi: 2, y_lo: 2; y = y_hi * 2 + y_lo), z: 32, core: 2. Of those that a mesh axis runs over, the one named last changes fastest.
Arguments:
- signal: bfloat16 [16384, 4096], P('ctx', 'tp'), may hold values from -6 to 6
- gate: bfloat16 [16384, 4096], P('ctx', 'tp'), may hold values from -6 to 6
- skip: float32 [4096], P('tp'), may hold values from -1 to 1
- filter_taps: bfloat16 [16384, 4096], P('ctx', 'tp'), may hold values from -0.046875 to 0.046875
- out_weight: bfloat16 [4096, 4096], P('tp'), may hold values from -0.125 to 0.125
Outputs:
- mixed_out: bfloat16 [16384, 4096], P('ctx', 'tp')
All inputs are finite; a program needn't handle non-finite values.
Results may differ from a plain program's by a relative error of at most 0.023.
Values may be sent and summed in bfloat16 or wider, within the bound.
No kernel may reach another device: no remote copies, remote signals or barrier semaphores. Data moves between devices by JAX's collectives and lax.ppermute only.
A program may use at most 64 MiB of HBM per device.

v0:
```python
import math

import jax
import jax.numpy as jnp
from jax import lax
from jax.sharding import PartitionSpec as P


def swapped(shard, axis, apart):
    return lax.ppermute(shard, axis, [(i, i ^ 1 << apart) for i in range(lax.axis_size(axis))])


def pair_up(real_part, imag_part, shape):
    return jnp.stack([real_part, imag_part], axis=1).reshape(shape)


def rotate(stack, cosine, sine):
    real_part = stack[0::2]
    imag_part = stack[1::2]
    return pair_up(
        real_part * cosine - imag_part * sine, real_part * sine + imag_part * cosine, stack.shape
    )


def multiply(stack, other):
    sr, si = (stack[0::2], stack[1::2])
    hr, hi = (other[0::2], other[1::2])
    return pair_up(sr * hr - si * hi, sr * hi + si * hr, stack.shape)


def start_panels(source, cosine, sine):
    return jnp.stack([source, jnp.zeros_like(source), source * cosine, source * sine])


def both_panels(source, taps, place, length):
    angle = place.astype(jnp.float32) * (-math.pi / length)
    cosine = jnp.cos(angle)[:, None]
    sine = jnp.sin(angle)[:, None]
    return jnp.concatenate([start_panels(source, cosine, sine), start_panels(taps, cosine, sine)])


def dft_tables(rows):
    local = jnp.arange(rows, dtype=jnp.int32)
    grid = local[:, None] * local[None, :] % rows
    angle = grid.astype(jnp.float32) * (-2.0 * math.pi / rows)
    return (jnp.cos(angle), jnp.sin(angle))


def block_transform(stack, table_re, table_im):
    with_re = jnp.einsum("jq,sjc->sqc", table_re, stack, precision=lax.Precision.HIGHEST)
    with_im = jnp.einsum("jq,sjc->sqc", table_im, stack, precision=lax.Precision.HIGHEST)
    return pair_up(with_re[0::2] - with_im[1::2], with_re[1::2] + with_im[0::2], stack.shape)


def per_device(signal, gate, skip, filter_taps, out_weight):
    rows = signal.shape[0]
    count = lax.axis_size("ctx")
    levels = count.bit_length() - 1
    length = rows * count
    source = signal.astype(jnp.float32)
    device = lax.axis_index("ctx")
    local = jnp.arange(rows, dtype=jnp.int32)
    place = device * rows + local
    state = both_panels(source, filter_taps.astype(jnp.float32), place, length)

    def level_turn(bit, sign):
        span = rows << bit
        offset = device % (1 << bit) * rows + local
        angle = offset.astype(jnp.float32) * (sign * math.pi / span)
        return (jnp.cos(angle)[:, None], jnp.sin(angle)[:, None])

    def upper_of(bit):
        return device >> bit & 1 == 1

    order = list(reversed(range(levels)))
    for bit in order:
        sent = state.astype(jnp.bfloat16)
        other = swapped(sent, "ctx", bit).astype(jnp.float32)
        forward_own = sent.astype(jnp.float32)
        forward_cosine, forward_sine = level_turn(bit, -1.0)
        state = jnp.where(
            upper_of(bit),
            rotate(other - forward_own, forward_cosine, forward_sine),
            forward_own + other,
        )
    table_re, table_im = dft_tables(rows)
    state = block_transform(state, table_re, table_im)
    state = multiply(state[:4], state[4:])
    state = block_transform(state, table_re, -table_im)
    for bit in range(levels):
        sent = state.astype(jnp.bfloat16)
        other = swapped(sent, "ctx", bit).astype(jnp.float32)
        own = sent.astype(jnp.float32)
        cosine, sine = level_turn(bit, 1.0)
        state = jnp.where(
            upper_of(bit), other - rotate(own, cosine, sine), own + rotate(other, cosine, sine)
        )
    start_angle = place.astype(jnp.float32) * (-math.pi / length)
    wr = jnp.cos(start_angle)[:, None]
    wi = jnp.sin(start_angle)[:, None]
    conv = (state[0] + wr * state[2] + wi * state[3]) / (2.0 * length)
    mixed = (gate.astype(jnp.float32) * (conv + skip[None, :] * source)).astype(jnp.bfloat16)
    partial_value = jnp.dot(mixed, out_weight, preferred_element_type=jnp.float32)
    return lax.psum_scatter(
        partial_value.astype(jnp.bfloat16), "tp", scatter_dimension=1, tiled=True
    )


def solution(mesh):
    return jax.shard_map(
        per_device,
        mesh=mesh,
        in_specs=(P("ctx", "tp"), P("ctx", "tp"), P("tp"), P("ctx", "tp"), P("tp", None)),
        out_specs=P("ctx", "tp"),
        check_vma=False,
    )
```

profile of v0, /device:TPU:1, one launch (start us, length us, event | category | flops | bytes accessed | tf_op | source)
XLA Modules:
  0.0 1041.5 jit_solution(3393029326784370279)
XLA Ops:
  12.4 29.5 %collective-permute-start = (bf16[8,128,512]{2,1,0:T(8,128)(2,1)S(1)}, bf16[8,128,512]{2,1,0:T(8,128)(2,1)S(1)}, u32[]{:S(2)}, u32[]{:S(2)}) collective-permute-start(bf16[8,128,512]{2,1,0:T(8,128)(2,1)S(1)} %fusion.47), channel_id=1, source_target_pairs={{0,512},{8,520},{16,528},{24,536},{32,544},{40,552},{48,560},{56,5... | collective-permute-start | bytes 3145736 | tf_op jit(solution)/shard_map/ppermute | solution.py:10
  42.0 44.3 %collective-permute-done = bf16[8,128,512]{2,1,0:T(8,128)(2,1)S(1)} collective-permute-done((bf16[8,128,512]{2,1,0:T(8,128)(2,1)S(1)}, bf16[8,128,512]{2,1,0:T(8,128)(2,1)S(1)}, u32[]{:S(2)}, u32[]{:S(2)}) %collective-permute-start) | collective-permute-done | bytes 1048608 | tf_op jit(solution)/shard_map/ppermute | solution.py:10
  87.8 111.5 %collective-permute-start.1 = (bf16[8,128,512]{2,1,0:T(8,128)(2,1)S(1)}, bf16[8,128,512]{2,1,0:T(8,128)(2,1)S(1)}, u32[]{:S(2)}, u32[]{:S(2)}) collective-permute-start(bf16[8,128,512]{2,1,0:T(8,128)(2,1)S(1)} %fusion.1), channel_id=1, source_target_pairs={{0,256},{8,264},{16,272},{24,280},{32,288},{40,296},{48,304},{56,3... | collective-permute-start | bytes 3145736 | tf_op jit(solution)/shard_map/ppermute | solution.py:10
  199.3 203.7 %collective-permute-done.1 = bf16[8,128,512]{2,1,0:T(8,128)(2,1)S(1)} collective-permute-done((bf16[8,128,512]{2,1,0:T(8,128)(2,1)S(1)}, bf16[8,128,512]{2,1,0:T(8,128)(2,1)S(1)}, u32[]{:S(2)}, u32[]{:S(2)}) %collective-permute-start.1) | collective-permute-done | bytes 1048608 | tf_op jit(solution)/shard_map/ppermute | solution.py:10
  406.5 86.7 %collective-permute-done.2 = bf16[8,128,512]{2,1,0:T(8,128)(2,1)S(1)} collective-permute-done((bf16[8,128,512]{2,1,0:T(8,128)(2,1)S(1)}, bf16[8,128,512]{2,1,0:T(8,128)(2,1)S(1)}, u32[]{:S(2)}, u32[]{:S(2)}) %collective-permute-start.2) | collective-permute-done | bytes 1048608 | tf_op jit(solution)/shard_map/ppermute | solution.py:10
  496.6 41.4 %collective-permute-done.3 = bf16[8,128,512]{2,1,0:T(8,128)(2,1)S(1)} collective-permute-done((bf16[8,128,512]{2,1,0:T(8,128)(2,1)S(1)}, bf16[8,128,512]{2,1,0:T(8,128)(2,1)S(1)}, u32[]{:S(2)}, u32[]{:S(2)}) %collective-permute-start.3) | collective-permute-done | bytes 1048608 | tf_op jit(solution)/shard_map/ppermute | solution.py:10
  541.5 24.1 %collective-permute-done.4 = bf16[8,128,512]{2,1,0:T(8,128)(2,1)S(1)} collective-permute-done((bf16[8,128,512]{2,1,0:T(8,128)(2,1)S(1)}, bf16[8,128,512]{2,1,0:T(8,128)(2,1)S(1)}, u32[]{:S(2)}, u32[]{:S(2)}) %collective-permute-start.4) | collective-permute-done | bytes 1048608 | tf_op jit(solution)/shard_map/ppermute | solution.py:10
  567.1 3.2 collective-permute-start.5
  570.4 21.9 %collective-permute-done.5 = bf16[8,128,512]{2,1,0:T(8,128)(2,1)S(1)} collective-permute-done((bf16[8,128,512]{2,1,0:T(8,128)(2,1)S(1)}, bf16[8,128,512]{2,1,0:T(8,128)(2,1)S(1)}, u32[]{:S(2)}, u32[]{:S(2)}) %collective-permute-start.5) | collective-permute-done | bytes 1048608 | tf_op jit(solution)/shard_map/ppermute | solution.py:10
  593.8 4.3 collective-permute-start.6
  601.9 3.6 convolution_bitcast_fusion
  605.5 3.6 convolution_bitcast_fusion.1
  613.9 2.3 collective-permute-start.7
  619.1 3.2 collective-permute-start.8
  622.4 11.8 %collective-permute-done.8 = bf16[4,128,512]{2,1,0:T(8,128)(2,1)S(1)} collective-permute-done((bf16[4,128,512]{2,1,0:T(8,128)(2,1)S(1)}, bf16[4,128,512]{2,1,0:T(8,128)(2,1)S(1)}, u32[]{:S(2)}, u32[]{:S(2)}) %collective-permute-start.8) | collective-permute-done | bytes 524320 | tf_op jit(solution)/shard_map/ppermute | solution.py:10
  635.5 2.2 collective-permute-start.9
  637.8 11.8 %collective-permute-done.9 = bf16[4,128,512]{2,1,0:T(8,128)(2,1)S(1)} collective-permute-done((bf16[4,128,512]{2,1,0:T(8,128)(2,1)S(1)}, bf16[4,128,512]{2,1,0:T(8,128)(2,1)S(1)}, u32[]{:S(2)}, u32[]{:S(2)}) %collective-permute-start.9) | collective-permute-done | bytes 524320 | tf_op jit(solution)/shard_map/ppermute | solution.py:10
  653.0 25.9 %collective-permute-done.10 = bf16[4,128,512]{2,1,0:T(8,128)(2,1)S(1)} collective-permute-done((bf16[4,128,512]{2,1,0:T(8,128)(2,1)S(1)}, bf16[4,128,512]{2,1,0:T(8,128)(2,1)S(1)}, u32[]{:S(2)}, u32[]{:S(2)}) %collective-permute-start.10) | collective-permute-done | bytes 524320 | tf_op jit(solution)/shard_map/ppermute | solution.py:10
  682.2 47.5 %collective-permute-done.11 = bf16[4,128,512]{2,1,0:T(8,128)(2,1)S(1)} collective-permute-done((bf16[4,128,512]{2,1,0:T(8,128)(2,1)S(1)}, bf16[4,128,512]{2,1,0:T(8,128)(2,1)S(1)}, u32[]{:S(2)}, u32[]{:S(2)}) %collective-permute-start.11) | collective-permute-done | bytes 524320 | tf_op jit(solution)/shard_map/ppermute | solution.py:10
  731.1 43.3 %collective-permute-start.12 = (bf16[4,128,512]{2,1,0:T(8,128)(2,1)S(1)}, bf16[4,128,512]{2,1,0:T(8,128)(2,1)S(1)}, u32[]{:S(2)}, u32[]{:S(2)}) collective-permute-start(bf16[4,128,512]{2,1,0:T(8,128)(2,1)S(1)} %get-tuple-element.8), channel_id=1, source_target_pairs={{0,256},{8,264},{16,272},{24,280},{32,288},{40,296},{48,304},{56,3... | collective-permute-start | bytes 1572872 | tf_op jit(solution)/shard_map/ppermute | solution.py:10
  774.4 75.2 %collective-permute-done.12 = bf16[4,128,512]{2,1,0:T(8,128)(2,1)S(1)} collective-permute-done((bf16[4,128,512]{2,1,0:T(8,128)(2,1)S(1)}, bf16[4,128,512]{2,1,0:T(8,128)(2,1)S(1)}, u32[]{:S(2)}, u32[]{:S(2)}) %collective-permute-start.12) | collective-permute-done | bytes 524320 | tf_op jit(solution)/shard_map/ppermute | solution.py:10
  851.0 28.4 %collective-permute-start.13 = (bf16[4,128,512]{2,1,0:T(8,128)(2,1)S(1)}, bf16[4,128,512]{2,1,0:T(8,128)(2,1)S(1)}, u32[]{:S(2)}, u32[]{:S(2)}) collective-permute-start(bf16[4,128,512]{2,1,0:T(8,128)(2,1)S(1)} %get-tuple-element.6), channel_id=1, source_target_pairs={{0,512},{8,520},{16,528},{24,536},{32,544},{40,552},{48,560},{56,5... | collective-permute-start | bytes 1572872 | tf_op jit(solution)/shard_map/ppermute | solution.py:10
  879.4 33.1 %collective-permute-done.13 = bf16[4,128,512]{2,1,0:T(8,128)(2,1)S(1)} collective-permute-done((bf16[4,128,512]{2,1,0:T(8,128)(2,1)S(1)}, bf16[4,128,512]{2,1,0:T(8,128)(2,1)S(1)}, u32[]{:S(2)}, u32[]{:S(2)}) %collective-permute-start.13) | collective-permute-done | bytes 524320 | tf_op jit(solution)/shard_map/ppermute | solution.py:10
  917.6 117.0 %reduce-scatter.2.cloned.1.call-done = bf16[128,512]{1,0:T(8,128)(2,1)} async-done(((bf16[128,4096]{1,0:T(8,128)(2,1)}), bf16[128,512]{1,0:T(8,128)(2,1)}) %reduce-scatter.2.cloned.1.call-update) | async-done | bytes 131088 | tf_op jit(solution)/shard_map/reduce_scatter | solution.py:104
  (138 shorter events, 47.5 us)
Async XLA Ops:
  6.5 1028.1 %reduce-scatter.2.cloned.1.call-start = ((), (), s32[]{:S(2)}) async-start(), calls=%async_computation.1 | async-start | bytes 1179648 | tf_op jit(solution)/shard_map/reduce_scatter | solution.py:104
  12.4 73.9 %collective-permute-start = (bf16[8,128,512]{2,1,0:T(8,128)(2,1)S(1)}, bf16[8,128,512]{2,1,0:T(8,128)(2,1)S(1)}, u32[]{:S(2)}, u32[]{:S(2)}) collective-permute-start(bf16[8,128,512]{2,1,0:T(8,128)(2,1)S(1)} %fusion.47), channel_id=1, source_target_pairs={{0,512},{8,520},{16,528},{24,536},{32,544},{40,552},{48,560},{56,5... | collective-permute-start | bytes 3145736 | tf_op jit(solution)/shard_map/ppermute | solution.py:10
  87.8 315.2 %collective-permute-start.1 = (bf16[8,128,512]{2,1,0:T(8,128)(2,1)S(1)}, bf16[8,128,512]{2,1,0:T(8,128)(2,1)S(1)}, u32[]{:S(2)}, u32[]{:S(2)}) collective-permute-start(bf16[8,128,512]{2,1,0:T(8,128)(2,1)S(1)} %fusion.1), channel_id=1, source_target_pairs={{0,256},{8,264},{16,272},{24,280},{32,288},{40,296},{48,304},{56,3... | collective-permute-start | bytes 3145736 | tf_op jit(solution)/shard_map/ppermute | solution.py:10
  404.5 88.7 %collective-permute-start.2 = (bf16[8,128,512]{2,1,0:T(8,128)(2,1)S(1)}, bf16[8,128,512]{2,1,0:T(8,128)(2,1)S(1)}, u32[]{:S(2)}, u32[]{:S(2)}) collective-permute-start(bf16[8,128,512]{2,1,0:T(8,128)(2,1)S(1)} %fusion.3), channel_id=1, source_target_pairs={{0,128},{8,136},{16,144},{24,152},{32,160},{40,168},{48,176},{56,1... | collective-permute-start | bytes 3145736 | tf_op jit(solution)/shard_map/ppermute | solution.py:10
  494.6 43.4 %collective-permute-start.3 = (bf16[8,128,512]{2,1,0:T(8,128)(2,1)S(1)}, bf16[8,128,512]{2,1,0:T(8,128)(2,1)S(1)}, u32[]{:S(2)}, u32[]{:S(2)}) collective-permute-start(bf16[8,128,512]{2,1,0:T(8,128)(2,1)S(1)} %fusion.5), channel_id=1, source_target_pairs={{0,64},{8,72},{16,80},{24,88},{32,96},{40,104},{48,112},{56,120},{... | collective-permute-start | bytes 3145736 | tf_op jit(solution)/shard_map/ppermute | solution.py:10
  539.5 26.1 %collective-permute-start.4 = (bf16[8,128,512]{2,1,0:T(8,128)(2,1)S(1)}, bf16[8,128,512]{2,1,0:T(8,128)(2,1)S(1)}, u32[]{:S(2)}, u32[]{:S(2)}) collective-permute-start(bf16[8,128,512]{2,1,0:T(8,128)(2,1)S(1)} %fusion.7), channel_id=1, source_target_pairs={{0,32},{8,40},{16,48},{24,56},{32,0},{40,8},{48,16},{56,24},{64,96... | collective-permute-start | bytes 3145736 | tf_op jit(solution)/shard_map/ppermute | solution.py:10
  567.1 25.2 %collective-permute-start.5 = (bf16[8,128,512]{2,1,0:T(8,128)(2,1)S(1)}, bf16[8,128,512]{2,1,0:T(8,128)(2,1)S(1)}, u32[]{:S(2)}, u32[]{:S(2)}) collective-permute-start(bf16[8,128,512]{2,1,0:T(8,128)(2,1)S(1)} %fusion.9), channel_id=1, source_target_pairs={{0,16},{8,24},{16,0},{24,8},{32,48},{40,56},{48,32},{56,40},{64,80... | collective-permute-start | bytes 3145736 | tf_op jit(solution)/shard_map/ppermute | solution.py:10
  593.8 6.4 collective-permute-start.6
  613.9 3.8 collective-permute-start.7
  619.1 15.0 %collective-permute-start.8 = (bf16[4,128,512]{2,1,0:T(8,128)(2,1)S(1)}, bf16[4,128,512]{2,1,0:T(8,128)(2,1)S(1)}, u32[]{:S(2)}, u32[]{:S(2)}) collective-permute-start(bf16[4,128,512]{2,1,0:T(8,128)(2,1)S(1)} %get-tuple-element.16), channel_id=1, source_target_pairs={{0,16},{8,24},{16,0},{24,8},{32,48},{40,56},{48,32},{56,40},{64,80... | collective-permute-start | bytes 1572872 | tf_op jit(solution)/shard_map/ppermute | solution.py:10
  635.5 14.1 %collective-permute-start.9 = (bf16[4,128,512]{2,1,0:T(8,128)(2,1)S(1)}, bf16[4,128,512]{2,1,0:T(8,128)(2,1)S(1)}, u32[]{:S(2)}, u32[]{:S(2)}) collective-permute-start(bf16[4,128,512]{2,1,0:T(8,128)(2,1)S(1)} %get-tuple-element.14), channel_id=1, source_target_pairs={{0,32},{8,40},{16,48},{24,56},{32,0},{40,8},{48,16},{56,24},{64,96... | collective-permute-start | bytes 1572872 | tf_op jit(solution)/shard_map/ppermute | solution.py:10
  651.0 27.8 %collective-permute-start.10 = (bf16[4,128,512]{2,1,0:T(8,128)(2,1)S(1)}, bf16[4,128,512]{2,1,0:T(8,128)(2,1)S(1)}, u32[]{:S(2)}, u32[]{:S(2)}) collective-permute-start(bf16[4,128,512]{2,1,0:T(8,128)(2,1)S(1)} %get-tuple-element.12), channel_id=1, source_target_pairs={{0,64},{8,72},{16,80},{24,88},{32,96},{40,104},{48,112},{56,120},{... | collective-permute-start | bytes 1572872 | tf_op jit(solution)/shard_map/ppermute | solution.py:10
  680.2 49.5 %collective-permute-start.11 = (bf16[4,128,512]{2,1,0:T(8,128)(2,1)S(1)}, bf16[4,128,512]{2,1,0:T(8,128)(2,1)S(1)}, u32[]{:S(2)}, u32[]{:S(2)}) collective-permute-start(bf16[4,128,512]{2,1,0:T(8,128)(2,1)S(1)} %get-tuple-element.10), channel_id=1, source_target_pairs={{0,128},{8,136},{16,144},{24,152},{32,160},{40,168},{48,176},{56,1... | collective-permute-start | bytes 1572872 | tf_op jit(solution)/shard_map/ppermute | solution.py:10
  731.1 118.5 %collective-permute-start.12 = (bf16[4,128,512]{2,1,0:T(8,128)(2,1)S(1)}, bf16[4,128,512]{2,1,0:T(8,128)(2,1)S(1)}, u32[]{:S(2)}, u32[]{:S(2)}) collective-permute-start(bf16[4,128,512]{2,1,0:T(8,128)(2,1)S(1)} %get-tuple-element.8), channel_id=1, source_target_pairs={{0,256},{8,264},{16,272},{24,280},{32,288},{40,296},{48,304},{56,3... | collective-permute-start | bytes 1572872 | tf_op jit(solution)/shard_map/ppermute | solution.py:10
  851.0 61.5 %collective-permute-start.13 = (bf16[4,128,512]{2,1,0:T(8,128)(2,1)S(1)}, bf16[4,128,512]{2,1,0:T(8,128)(2,1)S(1)}, u32[]{:S(2)}, u32[]{:S(2)}) collective-permute-start(bf16[4,128,512]{2,1,0:T(8,128)(2,1)S(1)} %get-tuple-element.6), channel_id=1, source_target_pairs={{0,512},{8,520},{16,528},{24,536},{32,544},{40,552},{48,560},{56,5... | collective-permute-start | bytes 1572872 | tf_op jit(solution)/shard_map/ppermute | solution.py:10
  913.3 0.9 copy-start.1
  913.3 1.0 copy-start.2
  913.3 1.0 copy-start.3
  913.5 2.2 copy-start
Sparse Core Ops, SparseCore 0:
  917.7 116.8 reduce-scatter.1
where the time goes:
time: 1040 us
  waiting for transfers between devices  748 us (72%)
  starting transfers between devices  237 us (23%)
  other arithmetic  22.9 us (2%)
  between operations  14.4 us (1%)
  matrix products  11.7 us (1%)
    ppermute x14, waiting for transfers between devices, swapped(): lax.ppermute(shard, axis, [(i, i ^ 1 << apart) for i in range(lax.axis_si...  631 us
    ppermute x14, starting transfers between devices, swapped(): lax.ppermute(shard, axis, [(i, i ^ 1 << apart) for i in range(lax.axis_si...  237 us
    reduce_scatter x1, waiting for transfers between devices, per_device(): lax.psum_scatter(partial_value.astype(jnp.bfloat16), 'tp', scatter_dimens...  117 us
  transfers between devices with their start and end apart: 15, of which 15 were waited for; matrix products, arithmetic and copies ran while one was open for 0% of the time, Pallas kernels for 0%

commit v1 on v0

v1 whole, which is shorter than its diff:
```python
import math

import jax
import jax.numpy as jnp
import numpy as np
from jax import lax
from jax.sharding import PartitionSpec as P

LANES = 128


def dft_table(rows, cols, size, sign):
    grid = np.arange(rows)[:, None] * np.arange(cols)[None, :] % size
    angle = grid * (sign * 2.0 * math.pi / size)
    return np.cos(angle), np.sin(angle)


def as_bf16(values):
    return jnp.asarray(values, jnp.float32).astype(jnp.bfloat16)


def mm(spec, table, data):
    return jnp.einsum(spec, table, data.astype(jnp.bfloat16), preferred_element_type=jnp.float32)


def long_conv(x, h, length):
    per = x.shape[0]
    half = length // LANES
    full = 2 * half
    total = 2 * length
    f1r, f1i = (as_bf16(t) for t in dft_table(full, half, full, -1.0))
    f3r, f3i = (as_bf16(t) for t in dft_table(LANES, LANES, LANES, -1.0))
    twr, twi = (jnp.asarray(t, jnp.float32) for t in dft_table(full, LANES, total, -1.0))
    both = jnp.concatenate([x.reshape(per, half, LANES), h.reshape(per, half, LANES)])
    ar = mm("kp,spq->skq", f1r, both)
    ai = mm("kp,spq->skq", f1i, both)
    br = ar * twr - ai * twi
    bi = ar * twi + ai * twr
    xr = mm("skq,qm->skm", br, f3r) - mm("skq,qm->skm", bi, f3i)
    xi = mm("skq,qm->skm", br, f3i) + mm("skq,qm->skm", bi, f3r)
    zr = xr[:per] * xr[per:] - xi[:per] * xi[per:]
    zi = xr[:per] * xi[per:] + xi[:per] * xr[per:]
    ur = mm("skq,qm->skm", zr, f3r) + mm("skq,qm->skm", zi, f3i)
    ui = mm("skq,qm->skm", zi, f3r) - mm("skq,qm->skm", zr, f3i)
    vr = ur * twr + ui * twi
    vi = ui * twr - ur * twi
    conv = mm("kp,skq->spq", f1r, vr) + mm("kp,skq->spq", f1i, vi)
    return conv.reshape(per, length) * (1.0 / total)


def per_device(signal, gate, skip, filter_taps, out_weight):
    rows, width = signal.shape
    count = lax.axis_size("ctx")
    length = rows * count
    per = width // count
    stack = jnp.stack([signal, filter_taps, gate]).transpose(0, 2, 1)
    gathered = lax.all_to_all(stack, "ctx", 1, 2, tiled=True)
    conv = long_conv(gathered[0], gathered[1], length)
    source = gathered[0].astype(jnp.float32)
    coeff = lax.dynamic_slice(skip, (lax.axis_index("ctx") * per,), (per,))
    mixed = (gathered[2].astype(jnp.float32) * (conv + coeff[:, None] * source)).astype(jnp.bfloat16)
    back = lax.all_to_all(mixed, "ctx", 1, 0, tiled=True)
    partial_value = jnp.einsum("cr,co->ro", back, out_weight, preferred_element_type=jnp.float32)
    return lax.psum_scatter(
        partial_value.astype(jnp.bfloat16), "tp", scatter_dimension=1, tiled=True
    )


def solution(mesh):
    return jax.shard_map(
        per_device,
        mesh=mesh,
        in_specs=(P("ctx", "tp"), P("ctx", "tp"), P("tp"), P("ctx", "tp"), P("tp", None)),
        out_specs=P("ctx", "tp"),
        check_vma=False,
    )
```

time: 1040 us -> 247 us (0.24)
  waiting for transfers between devices: 748 us -> 144 us
  starting transfers between devices: 237 us -> 32.4 us
  blocking collectives: 0 us -> 44.5 us
  other arithmetic: 22.9 us -> 1.27 us
    ppermute x14 -> x0, waiting for transfers between devices: 631 us -> none  [swapped(): lax.ppermute(shard, axis, [(i, i ^ 1 << apart) for i in range(lax.axis_si...]
    ppermute x14 -> x0, starting transfers between devices: 237 us -> none  [swapped(): lax.ppermute(shard, axis, [(i, i ^ 1 << apart) for i in range(lax.axis_si...]
    all_to_all x0 -> x1, waiting for transfers between devices: none -> 54.5 us  [per_device(): gathered = lax.all_to_all(stack, 'ctx', 1, 2, tiled=True)]
    all_to_all x0 -> x1, blocking collectives: none -> 44.5 us  [per_device(): back = lax.all_to_all(mixed, 'ctx', 1, 0, tiled=True)]
    all_to_all x0 -> x1, starting transfers between devices: none -> 32.3 us  [per_device(): gathered = lax.all_to_all(stack, 'ctx', 1, 2, tiled=True)]
    reduce_scatter x1, waiting for transfers between devices: 117 us -> 89.5 us  [per_device(): lax.psum_scatter(partial_value.astype(jnp.bfloat16), 'tp', scatter_dimens...]
  transfers between devices with their start and end apart: 15 -> 2, of which waited for: 15 -> 2; matrix products, arithmetic and copies ran while one was open for 0% -> 0% of each run, Pallas kernels for 0% -> 0%
where the time goes in v1:
time: 247 us; the launch traced here: 246 us
  waiting for transfers between devices  144 us (58%)
  blocking collectives  44.5 us (18%)
  starting transfers between devices  32.4 us (13%)
  between operations  13.6 us (6%)
  matrix products  7.4 us (3%)
    reduce_scatter x1, waiting for transfers between devices, per_device(): lax.psum_scatter(partial_value.astype(jnp.bfloat16), 'tp', scatter_dimens...  89.5 us
    all_to_all x1, waiting for transfers between devices, per_device(): gathered = lax.all_to_all(stack, 'ctx', 1, 2, tiled=True)  54.5 us
    all_to_all x1, blocking collectives, per_device(): back = lax.all_to_all(mixed, 'ctx', 1, 0, tiled=True)  44.5 us
    all_to_all x1, starting transfers between devices, per_device(): gathered = lax.all_to_all(stack, 'ctx', 1, 2, tiled=True)  32.3 us
  transfers between devices with their start and end apart: 2, of which 2 were waited for; matrix products, arithmetic and copies ran while one was open for 0% of the time, Pallas kernels for 0%

profile of v1, /device:TPU:1, one launch (start us, length us, event | category | flops | bytes accessed | tf_op | source)
XLA Modules:
  0.0 245.6 jit_solution(14198538936369943054)
XLA Ops:
  6.6 1.1 maximum_bitcast_fusion
  7.7 1.1 copy.47
  8.8 32.3 %all-to-all-start = ((bf16[3,512,128]{2,0,1:T(4,128)(2,1)}), bf16[3,512,128]{2,0,1:T(4,128)(2,1)S(1)}, u32[]{:S(2)}, u32[]{:S(2)}) async-start(bf16[3,512,128]{2,0,1:T(4,128)(2,1)} %copy.47), calls=%async_computation | async-start | bytes 1048576 | tf_op jit(solution)/shard_map/all_to_all | solution.py:57
  41.1 0.0 reduce-scatter.2.cloned.1.call-start
  41.1 0.8 dynamic_slice.3
  41.9 54.5 %all-to-all-done = bf16[3,512,128]{2,0,1:T(4,128)(2,1)S(1)} async-done(((bf16[3,512,128]{2,0,1:T(4,128)(2,1)}), bf16[3,512,128]{2,0,1:T(4,128)(2,1)S(1)}, u32[]{:S(2)}, u32[]{:S(2)}) %all-to-all-start) | async-done | bytes 393248 | tf_op jit(solution)/shard_map/all_to_all | solution.py:57
  96.4 0.4 copy.49
  96.9 0.3 convolution_bitcast_fusion.1
  97.2 0.3 convolution_bitcast_fusion
  97.5 0.4 fusion.6
  97.9 0.4 fusion.5
  98.2 0.4 convolution_subtract_fusion
  98.6 0.4 convolution_add_fusion
  99.0 0.1 multiply_subtract_fusion.1
  99.1 0.2 fusion.14
  99.4 0.2 fusion.15
  99.6 0.2 convolution_add_fusion.1
  99.8 0.2 convolution_subtract_fusion.1
  100.0 0.3 fusion.7
  100.3 0.3 fusion.4
  100.7 0.1 copy.58
  100.8 44.5 %all_to_all.31 = bf16[4,128,128]{2,0,1:T(4,128)(2,1)S(1)} all-to-all(bf16[4,128,128]{2,0,1:T(4,128)(2,1)S(1)} %copy.58), channel_id=1, replica_groups=mesh['ctx'=128,'tp'=8] {'ctx'}, dimensions={1} | all-to-all | bytes 262144 | tf_op jit(solution)/shard_map/all_to_all | solution.py:62
  145.3 3.9 %convolution_convert_fusion = bf16[128,4096]{1,0:T(8,128)(2,1)} fusion(bf16[512,128]{1,0:T(8,128)(2,1)S(1)} %bitcast.58, bf16[512,4096]{1,0:T(8,128)(2,1)} %param.15), kind=kOutput, calls=%fused_computation | convolution fusion | flops 537395200 | bytes 5373952 | tf_op jit(solution)/shard_map/cr,co->ro/dot_general | solution.py:63
  149.3 89.5 %reduce-scatter.2.cloned.1.call-done = bf16[128,512]{1,0:T(8,128)(2,1)} async-done(((bf16[128,4096]{1,0:T(8,128)(2,1)}), bf16[128,512]{1,0:T(8,128)(2,1)}) %reduce-scatter.2.cloned.1.call-update) | async-done | bytes 131088 | tf_op jit(solution)/shard_map/reduce_scatter | solution.py:64
  (18 shorter events, 0.1 us)
Async XLA Ops:
  6.5 90.3 %copy-start.7 = (bf16[256,128,1]{1,0,2:T(8,128)(2,1)S(1)}, bf16[256,128,1]{1,0,2:T(8,128)(2,1)}, u32[]{:S(2)}) copy-start(bf16[256,128,1]{1,0,2:T(8,128)(2,1)} %constant.36) | copy-start | bytes 196612
  6.5 90.6 %copy-start.6 = (bf16[256,128,1]{1,0,2:T(8,128)(2,1)S(1)}, bf16[256,128,1]{1,0,2:T(8,128)(2,1)}, u32[]{:S(2)}) copy-start(bf16[256,128,1]{1,0,2:T(8,128)(2,1)} %constant.37) | copy-start | bytes 196612
  6.5 90.9 %copy-start = (f32[256,128]{0,1:T(8,128)S(1)}, f32[256,128]{0,1:T(8,128)}, u32[]{:S(2)}) copy-start(f32[256,128]{0,1:T(8,128)} %constant.30.clone) | copy-start | bytes 393220
  6.5 90.9 %copy-start.1 = (f32[256,128]{0,1:T(8,128)S(1)}, f32[256,128]{0,1:T(8,128)}, u32[]{:S(2)}) copy-start(f32[256,128]{0,1:T(8,128)} %constant.31.clone) | copy-start | bytes 393220
  6.5 90.9 %copy-start.2 = (bf16[128,128,1]{1,0,2:T(8,128)(2,1)S(1)}, bf16[128,128,1]{1,0,2:T(8,128)(2,1)}, u32[]{:S(2)}) copy-start(bf16[128,128,1]{1,0,2:T(8,128)(2,1)} %constant.38) | copy-start | bytes 98308
  8.8 89.1 %copy-start.5 = (bf16[128,128,1]{1,0,2:T(8,128)(2,1)S(1)}, bf16[128,128,1]{1,0,2:T(8,128)(2,1)}, u32[]{:S(2)}) copy-start(bf16[128,128,1]{1,0,2:T(8,128)(2,1)} %constant.39) | copy-start | bytes 98308
  8.8 87.7 %all-to-all-start = ((bf16[3,512,128]{2,0,1:T(4,128)(2,1)}), bf16[3,512,128]{2,0,1:T(4,128)(2,1)S(1)}, u32[]{:S(2)}, u32[]{:S(2)}) async-start(bf16[3,512,128]{2,0,1:T(4,128)(2,1)} %copy.47), calls=%async_computation | async-start | bytes 1048576 | tf_op jit(solution)/shard_map/all_to_all | solution.py:57
  41.1 197.7 %reduce-scatter.2.cloned.1.call-start = ((), (), s32[]{:S(2)}) async-start(), calls=%async_computation.3 | async-start | bytes 1179648 | tf_op jit(solution)/shard_map/reduce_scatter | solution.py:64
  99.0 1.0 copy-start.3
  99.0 1.0 copy-start.4
Sparse Core Ops, SparseCore 0:
  149.4 89.3 reduce-scatter.1

commit v2 on v1

--- a/solution.py
+++ b/solution.py
@@ -61,9 +61,27 @@
     mixed = (gathered[2].astype(jnp.float32) * (conv + coeff[:, None] * source)).astype(jnp.bfloat16)
     back = lax.all_to_all(mixed, "ctx", 1, 0, tiled=True)
     partial_value = jnp.einsum("cr,co->ro", back, out_weight, preferred_element_type=jnp.float32)
-    return lax.psum_scatter(
-        partial_value.astype(jnp.bfloat16), "tp", scatter_dimension=1, tiled=True
-    )
+    return halving_scatter(partial_value.astype(jnp.bfloat16), "tp")
+
+
+def halving_scatter(value, axis):
+    count = lax.axis_size(axis)
+    index = lax.axis_index(axis)
+    rows, cols = value.shape
+    levels = count.bit_length() - 1
+    blocks = value.reshape(rows, *([2] * levels), cols // count)
+    total = None
+    for bit in range(levels):
+        dim = levels - bit
+        upper = (index >> bit & 1) == 1
+        low = lax.index_in_dim(blocks, 0, dim, keepdims=False)
+        high = lax.index_in_dim(blocks, 1, dim, keepdims=False)
+        keep = jnp.where(upper, high, low)
+        sent = jnp.where(upper, low, high)
+        got = lax.ppermute(sent, axis, [(i, i ^ 1 << bit) for i in range(count)])
+        total = keep.astype(jnp.float32) + got.astype(jnp.float32)
+        blocks = total.astype(jnp.bfloat16)
+    return total.reshape(rows, cols // count).astype(jnp.bfloat16)
 
 
 def solution(mesh):

time: 247 us -> 183 us (0.74)
  blocking collectives: 44.5 us -> 0 us
  waiting for transfers between devices: 144 us -> 106 us
  starting transfers between devices: 32.4 us -> 59.3 us
  between operations: 13.6 us -> 0.31 us
  local copies, waits for them, and re-layouts: 2.42 us -> 5.36 us
    reduce_scatter x1 -> x0, waiting for transfers between devices: 89.5 us -> none  [per_device(): lax.psum_scatter(partial_value.astype(jnp.bfloat16), 'tp', scatter_dimens...]
    all_to_all x1 -> x0, blocking collectives: 44.5 us -> none  [per_device(): back = lax.all_to_all(mixed, 'ctx', 1, 0, tiled=True)]
    all_to_all x0 -> x1, waiting for transfers between devices: none -> 29.8 us  [per_device(): back = lax.all_to_all(mixed, 'ctx', 1, 0, tiled=True)]
    ppermute x0 -> x3, waiting for transfers between devices: none -> 21.3 us  [halving_scatter(): got = lax.ppermute(sent, axis, [(i, i ^ 1 << bit) for i in range(count)])]
    all_to_all x0 -> x1, starting transfers between devices: none -> 14.8 us  [per_device(): back = lax.all_to_all(mixed, 'ctx', 1, 0, tiled=True)]
    ppermute x0 -> x3, starting transfers between devices: none -> 12.3 us  [halving_scatter(): got = lax.ppermute(sent, axis, [(i, i ^ 1 << bit) for i in range(count)])]
  transfers between devices with their start and end apart: 2 -> 5, of which waited for: 2 -> 5; matrix products, arithmetic and copies ran while one was open for 0% -> 0% of each run, Pallas kernels for 0% -> 0%
where the time goes in v2:
time: 183 us; the launch traced here: 181 us
  waiting for transfers between devices  106 us (58%)
  starting transfers between devices  59.3 us (32%)
  matrix products  6.42 us (4%)
  local copies, waits for them, and re-layouts  5.36 us (3%)
  other arithmetic  3.35 us (2%)
    all_to_all x1, waiting for transfers between devices, per_device(): gathered = lax.all_to_all(stack, 'ctx', 1, 2, tiled=True)  54.6 us
    all_to_all x1, starting transfers between devices, per_device(): gathered = lax.all_to_all(stack, 'ctx', 1, 2, tiled=True)  32.3 us
    all_to_all x1, waiting for transfers between devices, per_device(): back = lax.all_to_all(mixed, 'ctx', 1, 0, tiled=True)  29.8 us
    ppermute x3, waiting for transfers between devices, halving_scatter(): got = lax.ppermute(sent, axis, [(i, i ^ 1 << bit) for i in range(count)])  21.3 us
    all_to_all x1, starting transfers between devices, per_device(): back = lax.all_to_all(mixed, 'ctx', 1, 0, tiled=True)  14.8 us
    ppermute x3, starting transfers between devices, halving_scatter(): got = lax.ppermute(sent, axis, [(i, i ^ 1 << bit) for i in range(count)])  12.3 us
  transfers between devices with their start and end apart: 5, of which 5 were waited for; matrix products, arithmetic and copies ran while one was open for 0% of the time, Pallas kernels for 0%

profile of v2, /device:TPU:1, one launch (start us, length us, event | category | flops | bytes accessed | tf_op | source)
XLA Modules:
  0.0 180.5 jit_solution(864659703458848071)
XLA Ops:
  0.0 1.1 maximum_bitcast_fusion
  1.2 1.1 copy.53
  2.2 32.3 %all-to-all-start = ((bf16[3,512,128]{2,0,1:T(4,128)(2,1)}), bf16[3,512,128]{2,0,1:T(4,128)(2,1)S(1)}, u32[]{:S(2)}, u32[]{:S(2)}) async-start(bf16[3,512,128]{2,0,1:T(4,128)(2,1)} %copy.53), calls=%async_computation | async-start | bytes 1048576 | tf_op jit(solution)/shard_map/all_to_all | solution.py:57
  34.6 0.8 dynamic_slice.3
  35.3 54.6 %all-to-all-done = bf16[3,512,128]{2,0,1:T(4,128)(2,1)S(1)} async-done(((bf16[3,512,128]{2,0,1:T(4,128)(2,1)}), bf16[3,512,128]{2,0,1:T(4,128)(2,1)S(1)}, u32[]{:S(2)}, u32[]{:S(2)}) %all-to-all-start) | async-done | bytes 393248 | tf_op jit(solution)/shard_map/all_to_all | solution.py:57
  89.9 0.4 copy.55
  91.0 0.4 fusion.8
  91.3 0.4 fusion.7
  91.7 0.4 convolution_subtract_fusion
  94.1 0.8 copy.64
  94.9 14.8 %all-to-all-start.1 = ((bf16[4,128,128]{2,0,1:T(4,128)(2,1)}), bf16[4,128,128]{2,0,1:T(4,128)(2,1)S(1)}, u32[]{:S(2)}, u32[]{:S(2)}) async-start(bf16[4,128,128]{2,0,1:T(4,128)(2,1)} %copy.64), calls=%async_computation.1 | async-start | bytes 262144 | tf_op jit(solution)/shard_map/all_to_all | solution.py:62
  109.7 29.8 %all-to-all-done.1 = bf16[4,128,128]{2,0,1:T(4,128)(2,1)S(1)} async-done(((bf16[4,128,128]{2,0,1:T(4,128)(2,1)}), bf16[4,128,128]{2,0,1:T(4,128)(2,1)S(1)}, u32[]{:S(2)}, u32[]{:S(2)}) %all-to-all-start.1) | async-done | bytes 131104 | tf_op jit(solution)/shard_map/all_to_all | solution.py:62
  139.5 2.9 %convolution_convert_fusion = bf16[128,4096]{1,0:T(8,128)(2,1)S(1)} fusion(bf16[512,128]{1,0:T(8,128)(2,1)S(1)} %bitcast.73, bf16[512,4096]{1,0:T(8,128)(2,1)} %param.15), kind=kOutput, calls=%fused_computation | convolution fusion | flops 537395200 | bytes 5373952 | tf_op jit(solution)/shard_map/cr,co->ro/dot_general | solution.py:63
  142.5 0.8 reshape.44
  143.3 1.5 fusion.17
  144.8 0.6 select_bitcast_fusion
  145.4 3.1 %collective-permute-start = (bf16[128,2,2,512]{3,0,1,2:T(8,128)(2,1)S(1)}, bf16[128,2,2,512]{3,0,1,2:T(8,128)(2,1)S(1)}, u32[]{:S(2)}, u32[]{:S(2)}) collective-permute-start(bf16[128,2,2,512]{3,0,1,2:T(8,128)(2,1)S(1)} %select_bitcast_fusion), channel_id=1, source_target_pairs={{0,1},{1,0},{2,3},{3,2},{4,5},{5,4},{6,7},{7,6},{8,9},{9,8},{10,11... | collective-permute-start | bytes 1572872 | tf_op jit(solution)/shard_map/ppermute | solution.py:81
  148.5 12.6 %collective-permute-done = bf16[128,2,2,512]{3,0,1,2:T(8,128)(2,1)S(1)} collective-permute-done((bf16[128,2,2,512]{3,0,1,2:T(8,128)(2,1)S(1)}, bf16[128,2,2,512]{3,0,1,2:T(8,128)(2,1)S(1)}, u32[]{:S(2)}, u32[]{:S(2)}) %collective-permute-start) | collective-permute-done | bytes 524320 | tf_op jit(solution)/shard_map/ppermute | solution.py:81
  161.1 0.6 fusion.5
  161.7 4.6 %collective-permute-start.1 = (bf16[128,2,512]{2,0,1:T(8,128)(2,1)S(1)}, bf16[128,2,512]{2,0,1:T(8,128)(2,1)S(1)}, u32[]{:S(2)}, u32[]{:S(2)}) collective-permute-start(bf16[128,2,512]{2,0,1:T(8,128)(2,1)S(1)} %select_bitcast_fusion.1), channel_id=1, source_target_pairs={{0,2},{1,3},{2,0},{3,1},{4,6},{5,7},{6,4},{7,5},{8,10},{9,11},{10,... | collective-permute-start | bytes 786440 | tf_op jit(solution)/shard_map/ppermute | solution.py:81
  166.4 6.1 %collective-permute-done.1 = bf16[128,2,512]{2,0,1:T(8,128)(2,1)S(1)} collective-permute-done((bf16[128,2,512]{2,0,1:T(8,128)(2,1)S(1)}, bf16[128,2,512]{2,0,1:T(8,128)(2,1)S(1)}, u32[]{:S(2)}, u32[]{:S(2)}) %collective-permute-start.1) | collective-permute-done | bytes 262176 | tf_op jit(solution)/shard_map/ppermute | solution.py:81
  172.6 4.5 %collective-permute-start.2 = (bf16[128,512]{1,0:T(8,128)(2,1)S(1)}, bf16[128,512]{1,0:T(8,128)(2,1)S(1)}, u32[]{:S(2)}, u32[]{:S(2)}) collective-permute-start(bf16[128,512]{1,0:T(8,128)(2,1)S(1)} %select_bitcast_fusion.2), channel_id=1, source_target_pairs={{0,4},{1,5},{2,6},{3,7},{4,0},{5,1},{6,2},{7,3},{8,12},{9,13},{10,... | collective-permute-start | bytes 393224 | tf_op jit(solution)/shard_map/ppermute | solution.py:81
  177.1 2.7 %collective-permute-done.2 = bf16[128,512]{1,0:T(8,128)(2,1)S(1)} collective-permute-done((bf16[128,512]{1,0:T(8,128)(2,1)S(1)}, bf16[128,512]{1,0:T(8,128)(2,1)S(1)}, u32[]{:S(2)}, u32[]{:S(2)}) %collective-permute-start.2) | collective-permute-done | bytes 131104 | tf_op jit(solution)/shard_map/ppermute | solution.py:81
  179.8 0.7 fusion.10
  (30 shorter events, 2.8 us)
Async XLA Ops:
  0.0 90.3 %copy-start.7 = (bf16[256,128,1]{1,0,2:T(8,128)(2,1)S(1)}, bf16[256,128,1]{1,0,2:T(8,128)(2,1)}, u32[]{:S(2)}) copy-start(bf16[256,128,1]{1,0,2:T(8,128)(2,1)} %constant.43) | copy-start | bytes 196612
  0.0 90.6 %copy-start.6 = (bf16[256,128,1]{1,0,2:T(8,128)(2,1)S(1)}, bf16[256,128,1]{1,0,2:T(8,128)(2,1)}, u32[]{:S(2)}) copy-start(bf16[256,128,1]{1,0,2:T(8,128)(2,1)} %constant.44) | copy-start | bytes 196612
  0.0 90.9 %copy-start = (f32[256,128]{0,1:T(8,128)S(1)}, f32[256,128]{0,1:T(8,128)}, u32[]{:S(2)}) copy-start(f32[256,128]{0,1:T(8,128)} %constant.37.clone) | copy-start | bytes 393220
  0.0 90.9 %copy-start.1 = (f32[256,128]{0,1:T(8,128)S(1)}, f32[256,128]{0,1:T(8,128)}, u32[]{:S(2)}) copy-start(f32[256,128]{0,1:T(8,128)} %constant.38.clone) | copy-start | bytes 393220
  0.0 90.9 %copy-start.2 = (bf16[128,128,1]{1,0,2:T(8,128)(2,1)S(1)}, bf16[128,128,1]{1,0,2:T(8,128)(2,1)}, u32[]{:S(2)}) copy-start(bf16[128,128,1]{1,0,2:T(8,128)(2,1)} %constant.45) | copy-start | bytes 98308
  2.2 89.1 %copy-start.5 = (bf16[128,128,1]{1,0,2:T(8,128)(2,1)S(1)}, bf16[128,128,1]{1,0,2:T(8,128)(2,1)}, u32[]{:S(2)}) copy-start(bf16[128,128,1]{1,0,2:T(8,128)(2,1)} %constant.46) | copy-start | bytes 98308
  2.2 87.7 %all-to-all-start = ((bf16[3,512,128]{2,0,1:T(4,128)(2,1)}), bf16[3,512,128]{2,0,1:T(4,128)(2,1)S(1)}, u32[]{:S(2)}, u32[]{:S(2)}) async-start(bf16[3,512,128]{2,0,1:T(4,128)(2,1)} %copy.53), calls=%async_computation | async-start | bytes 1048576 | tf_op jit(solution)/shard_map/all_to_all | solution.py:57
  92.4 1.0 copy-start.3
  92.5 1.0 copy-start.4
  94.9 44.6 %all-to-all-start.1 = ((bf16[4,128,128]{2,0,1:T(4,128)(2,1)}), bf16[4,128,128]{2,0,1:T(4,128)(2,1)S(1)}, u32[]{:S(2)}, u32[]{:S(2)}) async-start(bf16[4,128,128]{2,0,1:T(4,128)(2,1)} %copy.64), calls=%async_computation.1 | async-start | bytes 262144 | tf_op jit(solution)/shard_map/all_to_all | solution.py:62
  145.4 15.7 %collective-permute-start = (bf16[128,2,2,512]{3,0,1,2:T(8,128)(2,1)S(1)}, bf16[128,2,2,512]{3,0,1,2:T(8,128)(2,1)S(1)}, u32[]{:S(2)}, u32[]{:S(2)}) collective-permute-start(bf16[128,2,2,512]{3,0,1,2:T(8,128)(2,1)S(1)} %select_bitcast_fusion), channel_id=1, source_target_pairs={{0,1},{1,0},{2,3},{3,2},{4,5},{5,4},{6,7},{7,6},{8,9},{9,8},{10,11... | collective-permute-start | bytes 1572872 | tf_op jit(solution)/shard_map/ppermute | solution.py:81
  161.7 10.7 %collective-permute-start.1 = (bf16[128,2,512]{2,0,1:T(8,128)(2,1)S(1)}, bf16[128,2,512]{2,0,1:T(8,128)(2,1)S(1)}, u32[]{:S(2)}, u32[]{:S(2)}) collective-permute-start(bf16[128,2,512]{2,0,1:T(8,128)(2,1)S(1)} %select_bitcast_fusion.1), channel_id=1, source_target_pairs={{0,2},{1,3},{2,0},{3,1},{4,6},{5,7},{6,4},{7,5},{8,10},{9,11},{10,... | collective-permute-start | bytes 786440 | tf_op jit(solution)/shard_map/ppermute | solution.py:81
  172.6 7.2 %collective-permute-start.2 = (bf16[128,512]{1,0:T(8,128)(2,1)S(1)}, bf16[128,512]{1,0:T(8,128)(2,1)S(1)}, u32[]{:S(2)}, u32[]{:S(2)}) collective-permute-start(bf16[128,512]{1,0:T(8,128)(2,1)S(1)} %select_bitcast_fusion.2), channel_id=1, source_target_pairs={{0,4},{1,5},{2,6},{3,7},{4,0},{5,1},{6,2},{7,3},{8,12},{9,13},{10,... | collective-permute-start | bytes 393224 | tf_op jit(solution)/shard_map/ppermute | solution.py:81

commit v3 on v2

--- a/solution.py
+++ b/solution.py
@@ -52,15 +52,13 @@
     rows, width = signal.shape
     count = lax.axis_size("ctx")
     length = rows * count
-    per = width // count
-    stack = jnp.stack([signal, filter_taps, gate]).transpose(0, 2, 1)
+    stack = jnp.stack([signal, filter_taps]).transpose(0, 2, 1)
     gathered = lax.all_to_all(stack, "ctx", 1, 2, tiled=True)
-    conv = long_conv(gathered[0], gathered[1], length)
-    source = gathered[0].astype(jnp.float32)
-    coeff = lax.dynamic_slice(skip, (lax.axis_index("ctx") * per,), (per,))
-    mixed = (gathered[2].astype(jnp.float32) * (conv + coeff[:, None] * source)).astype(jnp.bfloat16)
-    back = lax.all_to_all(mixed, "ctx", 1, 0, tiled=True)
-    partial_value = jnp.einsum("cr,co->ro", back, out_weight, preferred_element_type=jnp.float32)
+    conv = long_conv(gathered[0], gathered[1], length).astype(jnp.bfloat16)
+    back = lax.all_to_all(conv, "ctx", 1, 0, tiled=True).astype(jnp.float32).T
+    source = signal.astype(jnp.float32)
+    mixed = (gate.astype(jnp.float32) * (back + skip[None, :] * source)).astype(jnp.bfloat16)
+    partial_value = jnp.dot(mixed, out_weight, preferred_element_type=jnp.float32)
     return halving_scatter(partial_value.astype(jnp.bfloat16), "tp")
 
 

time: 183 us -> 161 us (0.88)
  blocking collectives: 0 us -> 70.7 us
  waiting for transfers between devices: 106 us -> 50.8 us
  starting transfers between devices: 59.3 us -> 21.2 us
    all_to_all x0 -> x1, blocking collectives: none -> 70.7 us  [per_device(): gathered = lax.all_to_all(stack, 'ctx', 1, 2, tiled=True)]
    all_to_all x2 -> x1, waiting for transfers between devices: 84.4 us -> 29.6 us  [per_device(): back = lax.all_to_all(conv, 'ctx', 1, 0, tiled=True).astype(jnp.float32).T]
    all_to_all x2 -> x1, starting transfers between devices: 47.1 us -> 8.87 us  [per_device(): back = lax.all_to_all(conv, 'ctx', 1, 0, tiled=True).astype(jnp.float32).T]
  transfers between devices with their start and end apart: 5 -> 4, of which waited for: 5 -> 4; matrix products, arithmetic and copies ran while one was open for 0% -> 0% of each run, Pallas kernels for 0% -> 0%
where the time goes in v3:
time: 161 us; the launch traced here: 158 us
  blocking collectives  70.7 us (44%)
  waiting for transfers between devices  50.8 us (32%)
  starting transfers between devices  21.2 us (13%)
  matrix products  8.18 us (5%)
  local copies, waits for them, and re-layouts  3.77 us (2%)
  other arithmetic  3.29 us (2%)
    all_to_all x1, blocking collectives, per_device(): gathered = lax.all_to_all(stack, 'ctx', 1, 2, tiled=True)  70.7 us
    all_to_all x1, waiting for transfers between devices, per_device(): back = lax.all_to_all(conv, 'ctx', 1, 0, tiled=True).astype(jnp.float32).T  29.6 us
    ppermute x3, waiting for transfers between devices, halving_scatter(): got = lax.ppermute(sent, axis, [(i, i ^ 1 << bit) for i in range(count)])  21.3 us
    ppermute x3, starting transfers between devices, halving_scatter(): got = lax.ppermute(sent, axis, [(i, i ^ 1 << bit) for i in range(count)])  12.3 us
    all_to_all x1, starting transfers between devices, per_device(): back = lax.all_to_all(conv, 'ctx', 1, 0, tiled=True).astype(jnp.float32).T  8.87 us
    dot_general x12, matrix products, mm(): jnp.einsum(spec, table, data.astype(jnp.bfloat16), preferred_element_type...  5.15 us
  transfers between devices with their start and end apart: 4, of which 4 were waited for; matrix products, arithmetic and copies ran while one was open for 0% of the time, Pallas kernels for 0%

profile of v3, /device:TPU:1, one launch (start us, length us, event | category | flops | bytes accessed | tf_op | source)
XLA Modules:
  0.0 158.4 jit_solution(8230975586421998403)
XLA Ops:
  0.0 1.0 maximum_bitcast_fusion
  1.2 70.7 %all_to_all.25 = bf16[2,512,128]{2,0,1:T(2,128)(2,1)S(1)} all-to-all(bf16[2,512,128]{2,0,1:T(2,128)(2,1)S(1)} %copy.56), channel_id=1, replica_groups=mesh['ctx'=128,'tp'=8] {'ctx'}, dimensions={1} | all-to-all | bytes 524288 | tf_op jit(solution)/shard_map/all_to_all | solution.py:56
  72.2 1.1 convolution_bitcast_fusion.1
  73.3 1.1 convolution_bitcast_fusion
  74.5 0.4 fusion.6
  74.9 0.4 fusion.5
  75.2 0.4 convolution_subtract_fusion
  75.6 0.4 convolution_add_fusion
  77.4 0.3 fusion.2
  77.7 0.8 copy.67
  78.5 8.9 %all-to-all-start.1 = ((bf16[4,128,128]{2,0,1:T(4,128)(2,1)}), bf16[4,128,128]{2,0,1:T(4,128)(2,1)S(1)}, u32[]{:S(2)}, u32[]{:S(2)}) async-start(bf16[4,128,128]{2,0,1:T(4,128)(2,1)} %copy.67), calls=%async_computation.1 | async-start | bytes 262144 | tf_op jit(solution)/shard_map/all_to_all | solution.py:58
  87.7 29.6 %all-to-all-done.1 = bf16[4,128,128]{2,0,1:T(4,128)(2,1)S(1)} async-done(((bf16[4,128,128]{2,0,1:T(4,128)(2,1)}), bf16[4,128,128]{2,0,1:T(4,128)(2,1)S(1)}, u32[]{:S(2)}, u32[]{:S(2)}) %all-to-all-start.1) | async-done | bytes 131104 | tf_op jit(solution)/shard_map/all_to_all | solution.py:58
  117.3 3.0 %convolution_convert_fusion = bf16[128,4096]{1,0:T(8,128)(2,1)S(1)} fusion(bf16[512,4096]{1,0:T(8,128)(2,1)} %param.15, f32[128,512]{0,1:T(8,128)S(1)} %bitcast.59, bf16[128,512]{0,1:T(8,128)(2,1)S(1)} %copy.68, bf16[128,512]{0,1:T(8,128)(2,1)S(1)} %copy.55, f32[512]{0:T(512)S(1)} %copy-done.10), kind=kOutput, calls=%fused_computation | convolution fusion | flops 537788416 | bytes 5769216 | tf_op jit(solution)/shard_map/dot_general | solution.py:61
  120.3 0.8 reshape.34
  121.2 1.5 fusion.16
  122.7 0.6 select_bitcast_fusion
  123.3 3.1 %collective-permute-start = (bf16[128,2,2,512]{3,0,1,2:T(8,128)(2,1)S(1)}, bf16[128,2,2,512]{3,0,1,2:T(8,128)(2,1)S(1)}, u32[]{:S(2)}, u32[]{:S(2)}) collective-permute-start(bf16[128,2,2,512]{3,0,1,2:T(8,128)(2,1)S(1)} %select_bitcast_fusion), channel_id=1, source_target_pairs={{0,1},{1,0},{2,3},{3,2},{4,5},{5,4},{6,7},{7,6},{8,9},{9,8},{10,11... | collective-permute-start | bytes 1572872 | tf_op jit(solution)/shard_map/ppermute | solution.py:79
  126.4 12.5 %collective-permute-done = bf16[128,2,2,512]{3,0,1,2:T(8,128)(2,1)S(1)} collective-permute-done((bf16[128,2,2,512]{3,0,1,2:T(8,128)(2,1)S(1)}, bf16[128,2,2,512]{3,0,1,2:T(8,128)(2,1)S(1)}, u32[]{:S(2)}, u32[]{:S(2)}) %collective-permute-start) | collective-permute-done | bytes 524320 | tf_op jit(solution)/shard_map/ppermute | solution.py:79
  138.9 0.6 fusion.3
  139.6 4.7 %collective-permute-start.1 = (bf16[128,2,512]{2,0,1:T(8,128)(2,1)S(1)}, bf16[128,2,512]{2,0,1:T(8,128)(2,1)S(1)}, u32[]{:S(2)}, u32[]{:S(2)}) collective-permute-start(bf16[128,2,512]{2,0,1:T(8,128)(2,1)S(1)} %select_bitcast_fusion.1), channel_id=1, source_target_pairs={{0,2},{1,3},{2,0},{3,1},{4,6},{5,7},{6,4},{7,5},{8,10},{9,11},{10,... | collective-permute-start | bytes 786440 | tf_op jit(solution)/shard_map/ppermute | solution.py:79
  144.3 6.0 %collective-permute-done.1 = bf16[128,2,512]{2,0,1:T(8,128)(2,1)S(1)} collective-permute-done((bf16[128,2,512]{2,0,1:T(8,128)(2,1)S(1)}, bf16[128,2,512]{2,0,1:T(8,128)(2,1)S(1)}, u32[]{:S(2)}, u32[]{:S(2)}) %collective-permute-start.1) | collective-permute-done | bytes 262176 | tf_op jit(solution)/shard_map/ppermute | solution.py:79
  150.4 4.5 %collective-permute-start.2 = (bf16[128,512]{1,0:T(8,128)(2,1)S(1)}, bf16[128,512]{1,0:T(8,128)(2,1)S(1)}, u32[]{:S(2)}, u32[]{:S(2)}) collective-permute-start(bf16[128,512]{1,0:T(8,128)(2,1)S(1)} %select_bitcast_fusion.2), channel_id=1, source_target_pairs={{0,4},{1,5},{2,6},{3,7},{4,0},{5,1},{6,2},{7,3},{8,12},{9,13},{10,... | collective-permute-start | bytes 393224 | tf_op jit(solution)/shard_map/ppermute | solution.py:79
  155.0 2.7 %collective-permute-done.2 = bf16[128,512]{1,0:T(8,128)(2,1)S(1)} collective-permute-done((bf16[128,512]{1,0:T(8,128)(2,1)S(1)}, bf16[128,512]{1,0:T(8,128)(2,1)S(1)}, u32[]{:S(2)}, u32[]{:S(2)}) %collective-permute-start.2) | collective-permute-done | bytes 131104 | tf_op jit(solution)/shard_map/ppermute | solution.py:79
  157.7 0.7 fusion.8
  (37 shorter events, 2.1 us)
Async XLA Ops:
  0.0 74.5 %copy-start = (f32[256,128]{0,1:T(8,128)S(1)}, f32[256,128]{0,1:T(8,128)}, u32[]{:S(2)}) copy-start(f32[256,128]{0,1:T(8,128)} %constant.28.clone) | copy-start | bytes 393220
  0.0 74.5 %copy-start.1 = (f32[256,128]{0,1:T(8,128)S(1)}, f32[256,128]{0,1:T(8,128)}, u32[]{:S(2)}) copy-start(f32[256,128]{0,1:T(8,128)} %constant.29.clone) | copy-start | bytes 393220
  0.0 74.5 %copy-start.2 = (bf16[128,128,1]{1,0,2:T(8,128)(2,1)S(1)}, bf16[128,128,1]{1,0,2:T(8,128)(2,1)}, u32[]{:S(2)}) copy-start(bf16[128,128,1]{1,0,2:T(8,128)(2,1)} %constant.36) | copy-start | bytes 98308
  1.0 73.8 %copy-start.5 = (bf16[128,128,1]{1,0,2:T(8,128)(2,1)S(1)}, bf16[128,128,1]{1,0,2:T(8,128)(2,1)}, u32[]{:S(2)}) copy-start(bf16[128,128,1]{1,0,2:T(8,128)(2,1)} %constant.37) | copy-start | bytes 98308
  76.0 1.1 copy-start.3
  76.0 1.1 copy-start.4
  76.0 1.1 copy-start.8
  76.0 1.4 copy-start.7
  76.2 11.2 %copy-start.6 = (bf16[128,512]{1,0:T(8,128)(2,1)S(1)}, bf16[128,512]{1,0:T(8,128)(2,1)}, u32[]{:S(2)}) copy-start(bf16[128,512]{1,0:T(8,128)(2,1)} %param.11) | copy-start | bytes 393220
  76.2 11.4 %copy-start.9 = (bf16[128,512]{1,0:T(8,128)(2,1)S(1)}, bf16[128,512]{1,0:T(8,128)(2,1)}, u32[]{:S(2)}) copy-start(bf16[128,512]{1,0:T(8,128)(2,1)} %param.12) | copy-start | bytes 393220
  76.4 40.9 %copy-start.10 = (f32[512]{0:T(512)S(1)}, f32[512]{0:T(512)}, u32[]{:S(2)}) copy-start(f32[512]{0:T(512)} %param.13) | copy-start | bytes 6148
  78.5 38.7 %all-to-all-start.1 = ((bf16[4,128,128]{2,0,1:T(4,128)(2,1)}), bf16[4,128,128]{2,0,1:T(4,128)(2,1)S(1)}, u32[]{:S(2)}, u32[]{:S(2)}) async-start(bf16[4,128,128]{2,0,1:T(4,128)(2,1)} %copy.67), calls=%async_computation.1 | async-start | bytes 262144 | tf_op jit(solution)/shard_map/all_to_all | solution.py:58
  123.3 15.7 %collective-permute-start = (bf16[128,2,2,512]{3,0,1,2:T(8,128)(2,1)S(1)}, bf16[128,2,2,512]{3,0,1,2:T(8,128)(2,1)S(1)}, u32[]{:S(2)}, u32[]{:S(2)}) collective-permute-start(bf16[128,2,2,512]{3,0,1,2:T(8,128)(2,1)S(1)} %select_bitcast_fusion), channel_id=1, source_target_pairs={{0,1},{1,0},{2,3},{3,2},{4,5},{5,4},{6,7},{7,6},{8,9},{9,8},{10,11... | collective-permute-start | bytes 1572872 | tf_op jit(solution)/shard_map/ppermute | solution.py:79
  139.6 10.7 %collective-permute-start.1 = (bf16[128,2,512]{2,0,1:T(8,128)(2,1)S(1)}, bf16[128,2,512]{2,0,1:T(8,128)(2,1)S(1)}, u32[]{:S(2)}, u32[]{:S(2)}) collective-permute-start(bf16[128,2,512]{2,0,1:T(8,128)(2,1)S(1)} %select_bitcast_fusion.1), channel_id=1, source_target_pairs={{0,2},{1,3},{2,0},{3,1},{4,6},{5,7},{6,4},{7,5},{8,10},{9,11},{10,... | collective-permute-start | bytes 786440 | tf_op jit(solution)/shard_map/ppermute | solution.py:79
  150.4 7.2 %collective-permute-start.2 = (bf16[128,512]{1,0:T(8,128)(2,1)S(1)}, bf16[128,512]{1,0:T(8,128)(2,1)S(1)}, u32[]{:S(2)}, u32[]{:S(2)}) collective-permute-start(bf16[128,512]{1,0:T(8,128)(2,1)S(1)} %select_bitcast_fusion.2), channel_id=1, source_target_pairs={{0,4},{1,5},{2,6},{3,7},{4,0},{5,1},{6,2},{7,3},{8,12},{9,13},{10,... | collective-permute-start | bytes 393224 | tf_op jit(solution)/shard_map/ppermute | solution.py:79

commit v4 on v3

--- a/solution.py
+++ b/solution.py
@@ -59,27 +59,14 @@
     source = signal.astype(jnp.float32)
     mixed = (gate.astype(jnp.float32) * (back + skip[None, :] * source)).astype(jnp.bfloat16)
     partial_value = jnp.dot(mixed, out_weight, preferred_element_type=jnp.float32)
-    return halving_scatter(partial_value.astype(jnp.bfloat16), "tp")
+    return exchange_scatter(partial_value.astype(jnp.bfloat16), "tp")
 
 
-def halving_scatter(value, axis):
+def exchange_scatter(value, axis):
     count = lax.axis_size(axis)
-    index = lax.axis_index(axis)
     rows, cols = value.shape
-    levels = count.bit_length() - 1
-    blocks = value.reshape(rows, *([2] * levels), cols // count)
-    total = None
-    for bit in range(levels):
-        dim = levels - bit
-        upper = (index >> bit & 1) == 1
-        low = lax.index_in_dim(blocks, 0, dim, keepdims=False)
-        high = lax.index_in_dim(blocks, 1, dim, keepdims=False)
-        keep = jnp.where(upper, high, low)
-        sent = jnp.where(upper, low, high)
-        got = lax.ppermute(sent, axis, [(i, i ^ 1 << bit) for i in range(count)])
-        total = keep.astype(jnp.float32) + got.astype(jnp.float32)
-        blocks = total.astype(jnp.bfloat16)
-    return total.reshape(rows, cols // count).astype(jnp.bfloat16)
+    parts = lax.all_to_all(value.reshape(rows, count, cols // count), axis, 1, 1, tiled=True)
+    return parts.astype(jnp.float32).sum(1).astype(jnp.bfloat16)
 
 
 def solution(mesh):

time: 161 us -> 145 us (0.901); the launches traced: 158 us -> 145 us
  blocking collectives: 70.7 us -> 94.3 us
  waiting for transfers between devices: 50.8 us -> 29.6 us
  starting transfers between devices: 21.2 us -> 8.87 us
  local copies, waits for them, and re-layouts: 3.77 us -> 1.55 us
    all_to_all x0 -> x1, blocking collectives: none -> 23.6 us  [exchange_scatter(): lax.all_to_all(value.reshape(rows, count, cols // count), axis, 1, 1, til...]
    ppermute x3 -> x0, waiting for transfers between devices: 21.3 us -> none  [halving_scatter(): got = lax.ppermute(sent, axis, [(i, i ^ 1 << bit) for i in range(count)])]
    ppermute x3 -> x0, starting transfers between devices: 12.3 us -> none  [halving_scatter(): got = lax.ppermute(sent, axis, [(i, i ^ 1 << bit) for i in range(count)])]
  transfers between devices with their start and end apart: 4 -> 1, of which waited for: 4 -> 1; matrix products, arithmetic and copies ran while one was open for 0% -> 0% of each run, Pallas kernels for 0% -> 0%
where the time goes in v4:
time: 145 us
  blocking collectives  94.3 us (65%)
  waiting for transfers between devices  29.6 us (20%)
  starting transfers between devices  8.87 us (6%)
  matrix products  8.18 us (6%)
  other arithmetic  2.02 us (1%)
  local copies, waits for them, and re-layouts  1.55 us (1%)
    all_to_all x1, blocking collectives, per_device(): gathered = lax.all_to_all(stack, 'ctx', 1, 2, tiled=True)  70.7 us
    all_to_all x1, waiting for transfers between devices, per_device(): back = lax.all_to_all(conv, 'ctx', 1, 0, tiled=True).astype(jnp.float32).T  29.6 us
    all_to_all x1, blocking collectives, exchange_scatter(): lax.all_to_all(value.reshape(rows, count, cols // count), axis, 1, 1, til...  23.6 us
    all_to_all x1, starting transfers between devices, per_device(): back = lax.all_to_all(conv, 'ctx', 1, 0, tiled=True).astype(jnp.float32).T  8.87 us
    dot_general x12, matrix products, mm(): jnp.einsum(spec, table, data.astype(jnp.bfloat16), preferred_element_type...  5.15 us
    dot_general x1, matrix products, per_device(): jnp.dot(mixed, out_weight, preferred_element_type=jnp.float32)  3.04 us
  transfers between devices with their start and end apart: 1, of which 1 were waited for; matrix products, arithmetic and copies ran while one was open for 0% of the time, Pallas kernels for 0%

profile of v4, /device:TPU:1, one launch (start us, length us, event | category | flops | bytes accessed | tf_op | source)
XLA Modules:
  0.0 144.9 jit_solution(14012238140645180744)
XLA Ops:
  0.0 1.0 maximum_bitcast_fusion
  1.1 0.2 copy.51
  1.2 70.7 %all_to_all.30 = bf16[2,512,128]{2,0,1:T(2,128)(2,1)S(1)} all-to-all(bf16[2,512,128]{2,0,1:T(2,128)(2,1)S(1)} %copy.51), channel_id=1, replica_groups=mesh['ctx'=128,'tp'=8] {'ctx'}, dimensions={1} | all-to-all | bytes 524288 | tf_op jit(solution)/shard_map/all_to_all | solution.py:56
  72.0 0.2 copy.53
  72.2 1.1 convolution_bitcast_fusion.1
  73.3 1.1 convolution_bitcast_fusion
  74.5 0.4 fusion.4
  74.9 0.4 fusion.3
  75.2 0.4 convolution_subtract_fusion
  75.6 0.4 convolution_add_fusion
  76.0 0.1 multiply_subtract_fusion.1
  76.2 0.2 fusion.13
  76.4 0.2 fusion.14
  76.6 0.2 convolution_add_fusion.1
  76.9 0.2 convolution_subtract_fusion.1
  77.1 0.3 fusion.5
  77.4 0.3 fusion.2
  77.7 0.8 copy.62
  78.5 8.9 %all-to-all-start.1 = ((bf16[4,128,128]{2,0,1:T(4,128)(2,1)}), bf16[4,128,128]{2,0,1:T(4,128)(2,1)S(1)}, u32[]{:S(2)}, u32[]{:S(2)}) async-start(bf16[4,128,128]{2,0,1:T(4,128)(2,1)} %copy.62), calls=%async_computation.1 | async-start | bytes 262144 | tf_op jit(solution)/shard_map/all_to_all | solution.py:58
  87.4 0.1 copy.63
  87.7 29.6 %all-to-all-done.1 = bf16[4,128,128]{2,0,1:T(4,128)(2,1)S(1)} async-done(((bf16[4,128,128]{2,0,1:T(4,128)(2,1)}), bf16[4,128,128]{2,0,1:T(4,128)(2,1)S(1)}, u32[]{:S(2)}, u32[]{:S(2)}) %all-to-all-start.1) | async-done | bytes 131104 | tf_op jit(solution)/shard_map/all_to_all | solution.py:58
  117.3 3.0 %convolution_convert_fusion = bf16[128,4096]{1,0:T(8,128)(2,1)S(1)} fusion(bf16[512,4096]{1,0:T(8,128)(2,1)} %param.15, f32[128,512]{0,1:T(8,128)S(1)} %bitcast.50, bf16[128,512]{0,1:T(8,128)(2,1)S(1)} %copy.63, bf16[128,512]{0,1:T(8,128)(2,1)S(1)} %copy.50, f32[512]{0:T(512)S(1)} %copy-done.10), kind=kOutput, calls=%fused_computation | convolution fusion | flops 537788416 | bytes 5769216 | tf_op jit(solution)/shard_map/dot_general | solution.py:61
  120.4 23.6 %all_to_all.31 = bf16[128,8,512]{2,0,1:T(8,128)(2,1)S(1)} all-to-all(bf16[128,8,512]{2,0,1:T(8,128)(2,1)S(1)} %bitcast.46), channel_id=1, replica_groups=mesh['ctx'=128,'tp'=8] {'tp'}, dimensions={1} | all-to-all | bytes 2097152 | tf_op jit(solution)/shard_map/all_to_all | solution.py:68
  144.0 0.8 reduce_sum.12
  (26 shorter events, 0.3 us)
Async XLA Ops:
  0.0 74.5 %copy-start = (f32[256,128]{0,1:T(8,128)S(1)}, f32[256,128]{0,1:T(8,128)}, u32[]{:S(2)}) copy-start(f32[256,128]{0,1:T(8,128)} %constant.21.clone) | copy-start | bytes 393220
  0.0 74.5 %copy-start.1 = (f32[256,128]{0,1:T(8,128)S(1)}, f32[256,128]{0,1:T(8,128)}, u32[]{:S(2)}) copy-start(f32[256,128]{0,1:T(8,128)} %constant.22.clone) | copy-start | bytes 393220
  0.0 74.5 %copy-start.2 = (bf16[128,128,1]{1,0,2:T(8,128)(2,1)S(1)}, bf16[128,128,1]{1,0,2:T(8,128)(2,1)}, u32[]{:S(2)}) copy-start(bf16[128,128,1]{1,0,2:T(8,128)(2,1)} %constant.29) | copy-start | bytes 98308
  1.0 73.8 %copy-start.5 = (bf16[128,128,1]{1,0,2:T(8,128)(2,1)S(1)}, bf16[128,128,1]{1,0,2:T(8,128)(2,1)}, u32[]{:S(2)}) copy-start(bf16[128,128,1]{1,0,2:T(8,128)(2,1)} %constant.30) | copy-start | bytes 98308
  76.0 1.1 copy-start.3
  76.0 1.1 copy-start.4
  76.0 1.1 copy-start.8
  76.0 1.4 copy-start.7
  76.2 11.2 %copy-start.6 = (bf16[128,512]{1,0:T(8,128)(2,1)S(1)}, bf16[128,512]{1,0:T(8,128)(2,1)}, u32[]{:S(2)}) copy-start(bf16[128,512]{1,0:T(8,128)(2,1)} %param.11) | copy-start | bytes 393220
  76.2 11.4 %copy-start.9 = (bf16[128,512]{1,0:T(8,128)(2,1)S(1)}, bf16[128,512]{1,0:T(8,128)(2,1)}, u32[]{:S(2)}) copy-start(bf16[128,512]{1,0:T(8,128)(2,1)} %param.12) | copy-start | bytes 393220
  76.4 40.9 %copy-start.10 = (f32[512]{0:T(512)S(1)}, f32[512]{0:T(512)}, u32[]{:S(2)}) copy-start(f32[512]{0:T(512)} %param.13) | copy-start | bytes 6148
  78.5 38.7 %all-to-all-start.1 = ((bf16[4,128,128]{2,0,1:T(4,128)(2,1)}), bf16[4,128,128]{2,0,1:T(4,128)(2,1)S(1)}, u32[]{:S(2)}, u32[]{:S(2)}) async-start(bf16[4,128,128]{2,0,1:T(4,128)(2,1)} %copy.62), calls=%async_computation.1 | async-start | bytes 262144 | tf_op jit(solution)/shard_map/all_to_all | solution.py:58

commit v5 on v4

--- a/solution.py
+++ b/solution.py
@@ -28,23 +28,23 @@
     half = length // LANES
     full = 2 * half
     total = 2 * length
-    f1r, f1i = (as_bf16(t) for t in dft_table(full, half, full, -1.0))
-    f3r, f3i = (as_bf16(t) for t in dft_table(LANES, LANES, LANES, -1.0))
+    f1r, f1i = dft_table(full, half, full, -1.0)
+    f3r, f3i = dft_table(LANES, LANES, LANES, -1.0)
+    first = as_bf16(np.concatenate([f1r, f1i]))
+    third = as_bf16(np.block([[f3r, f3i], [-f3i, f3r]]))
     twr, twi = (jnp.asarray(t, jnp.float32) for t in dft_table(full, LANES, total, -1.0))
     both = jnp.concatenate([x.reshape(per, half, LANES), h.reshape(per, half, LANES)])
-    ar = mm("kp,spq->skq", f1r, both)
-    ai = mm("kp,spq->skq", f1i, both)
-    br = ar * twr - ai * twi
-    bi = ar * twi + ai * twr
-    xr = mm("skq,qm->skm", br, f3r) - mm("skq,qm->skm", bi, f3i)
-    xi = mm("skq,qm->skm", br, f3i) + mm("skq,qm->skm", bi, f3r)
-    zr = xr[:per] * xr[per:] - xi[:per] * xi[per:]
-    zi = xr[:per] * xi[per:] + xi[:per] * xr[per:]
-    ur = mm("skq,qm->skm", zr, f3r) + mm("skq,qm->skm", zi, f3i)
-    ui = mm("skq,qm->skm", zi, f3r) - mm("skq,qm->skm", zr, f3i)
-    vr = ur * twr + ui * twi
-    vi = ui * twr - ur * twi
-    conv = mm("kp,skq->spq", f1r, vr) + mm("kp,skq->spq", f1i, vi)
+    a = mm("kp,spq->skq", first, both)
+    ar, ai = a[:, :full], a[:, full:]
+    b = jnp.concatenate([ar * twr - ai * twi, ar * twi + ai * twr], axis=2)
+    spec = mm("skq,qm->skm", b, third)
+    xr, xi = spec[:per, :, :LANES], spec[:per, :, LANES:]
+    hr, hi = spec[per:, :, :LANES], spec[per:, :, LANES:]
+    z = jnp.concatenate([xr * hr - xi * hi, xr * hi + xi * hr], axis=2)
+    u = mm("skm,qm->skq", z, third)
+    ur, ui = u[:, :, :LANES], u[:, :, LANES:]
+    v = jnp.concatenate([ur * twr + ui * twi, ui * twr - ur * twi], axis=1)
+    conv = mm("kp,skq->spq", first, v)
     return conv.reshape(per, length) * (1.0 / total)
 
 

time: 145 us -> 143 us (0.986)
  matrix products: 8.18 us -> 4.61 us
    dot_general x12 -> x4, matrix products: 5.15 us -> 1.58 us  [mm(): jnp.einsum(spec, table, data.astype(jnp.bfloat16), preferred_element_type...]
where the time goes in v5:
time: 143 us
  blocking collectives  94.5 us (66%)
  waiting for transfers between devices  29.6 us (21%)
  starting transfers between devices  8.87 us (6%)
  matrix products  4.61 us (3%)
  local copies, waits for them, and re-layouts  2.52 us (2%)
  other arithmetic  2.5 us (2%)
    all_to_all x1, blocking collectives, per_device(): gathered = lax.all_to_all(stack, 'ctx', 1, 2, tiled=True)  70.9 us
    all_to_all x1, waiting for transfers between devices, per_device(): back = lax.all_to_all(conv, 'ctx', 1, 0, tiled=True).astype(jnp.float32).T  29.6 us
    all_to_all x1, blocking collectives, exchange_scatter(): lax.all_to_all(value.reshape(rows, count, cols // count), axis, 1, 1, til...  23.6 us
    all_to_all x1, starting transfers between devices, per_device(): back = lax.all_to_all(conv, 'ctx', 1, 0, tiled=True).astype(jnp.float32).T  8.87 us
    dot_general x1, matrix products, per_device(): jnp.dot(mixed, out_weight, preferred_element_type=jnp.float32)  3.03 us
  transfers between devices with their start and end apart: 1, of which 1 were waited for; matrix products, arithmetic and copies ran while one was open for 0% of the time, Pallas kernels for 0%

profile of v5, /device:TPU:1, one launch (start us, length us, event | category | flops | bytes accessed | tf_op | source)
XLA Modules:
  0.0 142.8 jit_solution(17911453032280999534)
XLA Ops:
  0.0 1.0 maximum_bitcast_fusion
  1.0 0.2 copy.43
  1.2 0.0 copy-start.6
  1.2 70.9 %all_to_all.30 = bf16[2,512,128]{2,0,1:T(2,128)(2,1)S(1)} all-to-all(bf16[2,512,128]{2,0,1:T(2,128)(2,1)S(1)} %copy.43), channel_id=1, replica_groups=mesh['ctx'=128,'tp'=8] {'ctx'}, dimensions={1} | all-to-all | bytes 524288 | tf_op jit(solution)/shard_map/all_to_all | solution.py:56
  72.1 0.2 copy.45
  72.3 0.4 convolution_bitcast_fusion
  72.8 0.3 multiply_subtract_fusion
  73.1 0.6 copy-done.1
  73.7 0.4 fusion
  74.2 0.2 multiply_subtract_fusion.1
  74.4 0.4 fusion.6
  74.7 0.3 copy-done.2
  75.1 0.1 copy-done.3
  75.1 0.1 add_convert_fusion
  75.3 0.3 fusion.5
  75.6 0.8 copy.52
  76.4 8.9 %all-to-all-start.1 = ((bf16[4,128,128]{2,0,1:T(4,128)(2,1)}), bf16[4,128,128]{2,0,1:T(4,128)(2,1)S(1)}, u32[]{:S(2)}, u32[]{:S(2)}) async-start(bf16[4,128,128]{2,0,1:T(4,128)(2,1)} %copy.52), calls=%async_computation.1 | async-start | bytes 262144 | tf_op jit(solution)/shard_map/all_to_all | solution.py:58
  85.3 0.1 copy.53
  85.4 0.1 copy.42
  85.6 29.6 %all-to-all-done.1 = bf16[4,128,128]{2,0,1:T(4,128)(2,1)S(1)} async-done(((bf16[4,128,128]{2,0,1:T(4,128)(2,1)}), bf16[4,128,128]{2,0,1:T(4,128)(2,1)S(1)}, u32[]{:S(2)}, u32[]{:S(2)}) %all-to-all-start.1) | async-done | bytes 131104 | tf_op jit(solution)/shard_map/all_to_all | solution.py:58
  115.2 3.0 %convolution_convert_fusion = bf16[128,4096]{1,0:T(8,128)(2,1)S(1)} fusion(bf16[512,4096]{1,0:T(8,128)(2,1)} %param.13, f32[128,512]{0,1:T(8,128)S(1)} %bitcast.35, bf16[128,512]{0,1:T(8,128)(2,1)S(1)} %copy.53, bf16[128,512]{0,1:T(8,128)(2,1)S(1)} %copy.42, f32[512]{0:T(512)S(1)} %copy-done.8), kind=kOutput, calls=%fused_computation | convolution fusion | flops 537788416 | bytes 5769216 | tf_op jit(solution)/shard_map/dot_general | solution.py:61
  118.2 0.1 copy.64
  118.3 23.6 %all_to_all.31 = bf16[128,8,512]{2,0,1:T(8,128)(2,1)S(1)} all-to-all(bf16[128,8,512]{2,0,1:T(8,128)(2,1)S(1)} %bitcast.31), channel_id=1, replica_groups=mesh['ctx'=128,'tp'=8] {'tp'}, dimensions={1} | all-to-all | bytes 2097152 | tf_op jit(solution)/shard_map/all_to_all | solution.py:68
  141.9 0.8 reduce_sum.12
  (16 shorter events, 0.1 us)
Async XLA Ops:
  0.0 72.3 %copy-start.4 = (bf16[512,128,1]{1,0,2:T(8,128)(2,1)S(1)}, bf16[512,128,1]{1,0,2:T(8,128)(2,1)}, u32[]{:S(2)}) copy-start(bf16[512,128,1]{1,0,2:T(8,128)(2,1)} %constant.19) | copy-start | bytes 393220
  1.2 71.6 %copy-start.6 = (f32[256,128]{0,1:T(8,128)S(1)}, f32[256,128]{0,1:T(8,128)}, u32[]{:S(2)}) copy-start(f32[256,128]{0,1:T(8,128)} %constant.15.clone) | copy-start | bytes 393220
  1.2 71.6 %copy-start.7 = (f32[256,128]{0,1:T(8,128)S(1)}, f32[256,128]{0,1:T(8,128)}, u32[]{:S(2)}) copy-start(f32[256,128]{0,1:T(8,128)} %constant.16.clone) | copy-start | bytes 393220
  72.8 0.9 copy-start.1
  74.2 0.9 copy-start.2
  74.2 1.0 copy-start.3
  75.1 10.2 %copy-start = (bf16[128,512]{1,0:T(8,128)(2,1)S(1)}, bf16[128,512]{1,0:T(8,128)(2,1)}, u32[]{:S(2)}) copy-start(bf16[128,512]{1,0:T(8,128)(2,1)} %param.9) | copy-start | bytes 393220
  75.1 10.3 %copy-start.5 = (bf16[128,512]{1,0:T(8,128)(2,1)S(1)}, bf16[128,512]{1,0:T(8,128)(2,1)}, u32[]{:S(2)}) copy-start(bf16[128,512]{1,0:T(8,128)(2,1)} %param.10) | copy-start | bytes 393220
  75.1 40.1 %copy-start.8 = (f32[512]{0:T(512)S(1)}, f32[512]{0:T(512)}, u32[]{:S(2)}) copy-start(f32[512]{0:T(512)} %param.11) | copy-start | bytes 6148
  76.4 38.7 %all-to-all-start.1 = ((bf16[4,128,128]{2,0,1:T(4,128)(2,1)}), bf16[4,128,128]{2,0,1:T(4,128)(2,1)S(1)}, u32[]{:S(2)}, u32[]{:S(2)}) async-start(bf16[4,128,128]{2,0,1:T(4,128)(2,1)} %copy.52), calls=%async_computation.1 | async-start | bytes 262144 | tf_op jit(solution)/shard_map/all_to_all | solution.py:58

commit v6 on v5

--- a/solution.py
+++ b/solution.py
@@ -55,18 +55,18 @@
     stack = jnp.stack([signal, filter_taps]).transpose(0, 2, 1)
     gathered = lax.all_to_all(stack, "ctx", 1, 2, tiled=True)
     conv = long_conv(gathered[0], gathered[1], length).astype(jnp.bfloat16)
-    back = lax.all_to_all(conv, "ctx", 1, 0, tiled=True).astype(jnp.float32).T
-    source = signal.astype(jnp.float32)
-    mixed = (gate.astype(jnp.float32) * (back + skip[None, :] * source)).astype(jnp.bfloat16)
-    partial_value = jnp.dot(mixed, out_weight, preferred_element_type=jnp.float32)
-    return exchange_scatter(partial_value.astype(jnp.bfloat16), "tp")
+    back = lax.all_to_all(conv, "ctx", 1, 0, tiled=True).astype(jnp.float32)
+    source = signal.T.astype(jnp.float32)
+    mixed = (gate.T.astype(jnp.float32) * (back + skip[:, None] * source)).astype(jnp.bfloat16)
+    partial_value = jnp.einsum("co,ct->ot", out_weight, mixed, preferred_element_type=jnp.float32)
+    return exchange_scatter(partial_value.astype(jnp.bfloat16), "tp").T
 
 
 def exchange_scatter(value, axis):
     count = lax.axis_size(axis)
     rows, cols = value.shape
-    parts = lax.all_to_all(value.reshape(rows, count, cols // count), axis, 1, 1, tiled=True)
-    return parts.astype(jnp.float32).sum(1).astype(jnp.bfloat16)
+    parts = lax.all_to_all(value.reshape(count, rows // count, cols), axis, 0, 0, tiled=True)
+    return parts.astype(jnp.float32).sum(0).astype(jnp.bfloat16)
 
 
 def solution(mesh):

time: 143 us -> 143 us (level)
  no operation moved by 1% of the time
where the time goes in v6:
time: 143 us
  blocking collectives  94.5 us (66%)
  waiting for transfers between devices  29.6 us (21%)
  starting transfers between devices  8.87 us (6%)
  matrix products  4.61 us (3%)
  local copies, waits for them, and re-layouts  2.52 us (2%)
  other arithmetic  2.5 us (2%)
    all_to_all x1, blocking collectives, per_device(): gathered = lax.all_to_all(stack, 'ctx', 1, 2, tiled=True)  70.9 us
    all_to_all x1, waiting for transfers between devices, per_device(): back = lax.all_to_all(conv, 'ctx', 1, 0, tiled=True).astype(jnp.float32)  29.6 us
    all_to_all x1, blocking collectives, exchange_scatter(): lax.all_to_all(value.reshape(count, rows // count, cols), axis, 0, 0, til...  23.6 us
    all_to_all x1, starting transfers between devices, per_device(): back = lax.all_to_all(conv, 'ctx', 1, 0, tiled=True).astype(jnp.float32)  8.87 us
    dot_general x1, matrix products, per_device(): jnp.einsum('co,ct->ot', out_weight, mixed, preferred_element_type=jnp.flo...  3.03 us
  transfers between devices with their start and end apart: 1, of which 1 were waited for; matrix products, arithmetic and copies ran while one was open for 0% of the time, Pallas kernels for 0%

profile of v6, /device:TPU:1, one launch (start us, length us, event | category | flops | bytes accessed | tf_op | source)
XLA Modules:
  0.0 142.8 jit_solution(3604099548304879380)
XLA Ops:
  0.0 1.0 maximum_bitcast_fusion
  1.0 0.2 copy.43
  1.2 0.0 copy-start.7
  1.2 70.9 %all_to_all.30 = bf16[2,512,128]{2,0,1:T(2,128)(2,1)S(1)} all-to-all(bf16[2,512,128]{2,0,1:T(2,128)(2,1)S(1)} %copy.43), channel_id=1, replica_groups=mesh['ctx'=128,'tp'=8] {'ctx'}, dimensions={1} | all-to-all | bytes 524288 | tf_op jit(solution)/shard_map/all_to_all | solution.py:56
  72.1 0.2 copy.45
  72.3 0.4 convolution_bitcast_fusion
  72.8 0.3 multiply_subtract_fusion
  73.1 0.6 copy-done.1
  73.7 0.4 fusion
  74.2 0.2 multiply_subtract_fusion.1
  74.4 0.4 fusion.6
  74.7 0.3 copy-done.2
  75.1 0.1 copy-done.3
  75.1 0.1 add_convert_fusion
  75.3 0.3 fusion.5
  75.6 0.8 copy.52
  76.4 8.9 %all-to-all-start.1 = ((bf16[4,128,128]{2,0,1:T(4,128)(2,1)}), bf16[4,128,128]{2,0,1:T(4,128)(2,1)S(1)}, u32[]{:S(2)}, u32[]{:S(2)}) async-start(bf16[4,128,128]{2,0,1:T(4,128)(2,1)} %copy.52), calls=%async_computation.1 | async-start | bytes 262144 | tf_op jit(solution)/shard_map/all_to_all | solution.py:58
  85.3 0.1 copy.53
  85.4 0.1 copy.42
  85.6 29.6 %all-to-all-done.1 = bf16[4,128,128]{2,0,1:T(4,128)(2,1)S(1)} async-done(((bf16[4,128,128]{2,0,1:T(4,128)(2,1)}), bf16[4,128,128]{2,0,1:T(4,128)(2,1)S(1)}, u32[]{:S(2)}, u32[]{:S(2)}) %all-to-all-start.1) | async-done | bytes 131104 | tf_op jit(solution)/shard_map/all_to_all | solution.py:58
  115.2 3.0 %convolution_convert_fusion = bf16[128,4096]{1,0:T(8,128)(2,1)S(1)} fusion(bf16[512,4096]{1,0:T(8,128)(2,1)} %param.13, f32[512,128]{1,0:T(8,128)S(1)} %bitcast.45, bf16[128,512]{0,1:T(8,128)(2,1)S(1)} %copy.42, bf16[128,512]{0,1:T(8,128)(2,1)S(1)} %copy.53, f32[512]{0:T(512)S(1)} %copy-done.8), kind=kOutput, calls=%fused_computation | convolution fusion | flops 537788416 | bytes 5769216 | tf_op jit(solution)/shard_map/co,ct->ot/dot_general | solution.py:61
  118.2 0.1 copy.64
  118.3 23.6 %all_to_all.31 = bf16[8,512,128]{1,2,0:T(8,128)(2,1)S(1)} all-to-all(bf16[8,512,128]{1,2,0:T(8,128)(2,1)S(1)} %bitcast.41), channel_id=1, replica_groups=mesh['ctx'=128,'tp'=8] {'tp'}, dimensions={0} | all-to-all | bytes 2097152 | tf_op jit(solution)/shard_map/all_to_all | solution.py:68
  141.9 0.8 reduce_sum.12
  (16 shorter events, 0.1 us)
Async XLA Ops:
  0.0 72.3 %copy-start.4 = (bf16[512,128,1]{1,0,2:T(8,128)(2,1)S(1)}, bf16[512,128,1]{1,0,2:T(8,128)(2,1)}, u32[]{:S(2)}) copy-start(bf16[512,128,1]{1,0,2:T(8,128)(2,1)} %constant.19) | copy-start | bytes 393220
  1.2 71.6 %copy-start.6 = (f32[256,128]{0,1:T(8,128)S(1)}, f32[256,128]{0,1:T(8,128)}, u32[]{:S(2)}) copy-start(f32[256,128]{0,1:T(8,128)} %constant.15.clone) | copy-start | bytes 393220
  1.2 71.6 %copy-start.7 = (f32[256,128]{0,1:T(8,128)S(1)}, f32[256,128]{0,1:T(8,128)}, u32[]{:S(2)}) copy-start(f32[256,128]{0,1:T(8,128)} %constant.16.clone) | copy-start | bytes 393220
  72.8 0.9 copy-start.1
  74.2 0.9 copy-start.2
  74.2 1.0 copy-start.3
  75.1 10.2 %copy-start = (bf16[128,512]{1,0:T(8,128)(2,1)S(1)}, bf16[128,512]{1,0:T(8,128)(2,1)}, u32[]{:S(2)}) copy-start(bf16[128,512]{1,0:T(8,128)(2,1)} %param.9) | copy-start | bytes 393220
  75.1 10.3 %copy-start.5 = (bf16[128,512]{1,0:T(8,128)(2,1)S(1)}, bf16[128,512]{1,0:T(8,128)(2,1)}, u32[]{:S(2)}) copy-start(bf16[128,512]{1,0:T(8,128)(2,1)} %param.10) | copy-start | bytes 393220
  75.1 40.1 %copy-start.8 = (f32[512]{0:T(512)S(1)}, f32[512]{0:T(512)}, u32[]{:S(2)}) copy-start(f32[512]{0:T(512)} %param.11) | copy-start | bytes 6148
  76.4 38.7 %all-to-all-start.1 = ((bf16[4,128,128]{2,0,1:T(4,128)(2,1)}), bf16[4,128,128]{2,0,1:T(4,128)(2,1)S(1)}, u32[]{:S(2)}, u32[]{:S(2)}) async-start(bf16[4,128,128]{2,0,1:T(4,128)(2,1)} %copy.52), calls=%async_computation.1 | async-start | bytes 262144 | tf_op jit(solution)/shard_map/all_to_all | solution.py:58

commit v7 on v6

--- a/solution.py
+++ b/solution.py
@@ -44,8 +44,8 @@
     u = mm("skm,qm->skq", z, third)
     ur, ui = u[:, :, :LANES], u[:, :, LANES:]
     v = jnp.concatenate([ur * twr + ui * twi, ui * twr - ur * twi], axis=1)
-    conv = mm("kp,skq->spq", first, v)
-    return conv.reshape(per, length) * (1.0 / total)
+    last = as_bf16(np.concatenate([f1r, f1i]) / total)
+    return mm("kp,skq->psq", last, v)
 
 
 def per_device(signal, gate, skip, filter_taps, out_weight):
@@ -55,7 +55,7 @@
     stack = jnp.stack([signal, filter_taps]).transpose(0, 2, 1)
     gathered = lax.all_to_all(stack, "ctx", 1, 2, tiled=True)
     conv = long_conv(gathered[0], gathered[1], length).astype(jnp.bfloat16)
-    back = lax.all_to_all(conv, "ctx", 1, 0, tiled=True).astype(jnp.float32)
+    back = lax.all_to_all(conv, "ctx", 0, 0, tiled=True).reshape(width, rows).astype(jnp.float32)
     source = signal.T.astype(jnp.float32)
     mixed = (gate.T.astype(jnp.float32) * (back + skip[:, None] * source)).astype(jnp.bfloat16)
     partial_value = jnp.einsum("co,ct->ot", out_weight, mixed, preferred_element_type=jnp.float32)

time: 143 us -> 143 us (level)
  no operation moved by 1% of the time
where the time goes in v7:
time: 143 us
  blocking collectives  94.5 us (66%)
  waiting for transfers between devices  29.6 us (21%)
  starting transfers between devices  8.87 us (6%)
  matrix products  4.59 us (3%)
  local copies, waits for them, and re-layouts  2.53 us (2%)
  other arithmetic  2.46 us (2%)
    all_to_all x1, blocking collectives, per_device(): gathered = lax.all_to_all(stack, 'ctx', 1, 2, tiled=True)  70.9 us
    all_to_all x1, waiting for transfers between devices, per_device(): lax.all_to_all(conv, 'ctx', 0, 0, tiled=True).reshape(width, rows)  29.6 us
    all_to_all x1, blocking collectives, exchange_scatter(): lax.all_to_all(value.reshape(count, rows // count, cols), axis, 0, 0, til...  23.6 us
    all_to_all x1, starting transfers between devices, per_device(): lax.all_to_all(conv, 'ctx', 0, 0, tiled=True).reshape(width, rows)  8.87 us
    dot_general x1, matrix products, per_device(): jnp.einsum('co,ct->ot', out_weight, mixed, preferred_element_type=jnp.flo...  3.02 us
  transfers between devices with their start and end apart: 1, of which 1 were waited for; matrix products, arithmetic and copies ran while one was open for 0% of the time, Pallas kernels for 0%

profile of v7, /device:TPU:1, one launch (start us, length us, event | category | flops | bytes accessed | tf_op | source)
XLA Modules:
  0.0 142.7 jit_solution(8699121222168417333)
XLA Ops:
  0.0 1.0 maximum_bitcast_fusion
  1.0 0.2 copy.44
  1.2 70.9 %all_to_all.25 = bf16[2,512,128]{2,0,1:T(2,128)(2,1)S(1)} all-to-all(bf16[2,512,128]{2,0,1:T(2,128)(2,1)S(1)} %copy.44), channel_id=1, replica_groups=mesh['ctx'=128,'tp'=8] {'ctx'}, dimensions={1} | all-to-all | bytes 524288 | tf_op jit(solution)/shard_map/all_to_all | solution.py:56
  72.1 0.2 copy.46
  72.3 0.4 convolution_bitcast_fusion
  72.8 0.3 multiply_subtract_fusion
  73.1 0.6 copy-done.1
  73.7 0.4 fusion
  74.2 0.2 multiply_subtract_fusion.1
  74.4 0.4 fusion.5
  74.7 0.3 copy-done.2
  75.1 0.1 copy-done.3
  75.1 0.1 add_convert_fusion
  75.3 0.0 copy-done.9
  75.3 0.3 fusion.4
  75.6 0.8 copy.53
  76.4 8.9 %all-to-all-start.1 = ((bf16[128,4,128]{2,1,0:T(4,128)(2,1)}), bf16[128,4,128]{2,1,0:T(4,128)(2,1)S(1)}, u32[]{:S(2)}, u32[]{:S(2)}) async-start(bf16[128,4,128]{2,1,0:T(4,128)(2,1)} %copy.53), calls=%async_computation.1 | async-start | bytes 262144 | tf_op jit(solution)/shard_map/all_to_all | solution.py:58
  85.3 0.1 copy.54
  85.5 0.1 copy.43
  85.6 29.6 %all-to-all-done.1 = bf16[128,4,128]{2,1,0:T(4,128)(2,1)S(1)} async-done(((bf16[128,4,128]{2,1,0:T(4,128)(2,1)}), bf16[128,4,128]{2,1,0:T(4,128)(2,1)S(1)}, u32[]{:S(2)}, u32[]{:S(2)}) %all-to-all-start.1) | async-done | bytes 131104 | tf_op jit(solution)/shard_map/all_to_all | solution.py:58
  115.2 3.0 %convolution_convert_fusion = bf16[128,4096]{1,0:T(8,128)(2,1)S(1)} fusion(bf16[512,4096]{1,0:T(8,128)(2,1)} %param.14, bf16[512,128]{1,0:T(8,128)(2,1)S(1)} %bitcast.41, bf16[128,512]{0,1:T(8,128)(2,1)S(1)} %copy.43, bf16[128,512]{0,1:T(8,128)(2,1)S(1)} %copy.54, f32[512]{0:T(512)S(1)} %copy-done.8), kind=kOutput, calls=%fused_computation | convolution fusion | flops 537853952 | bytes 5638144 | tf_op jit(solution)/shard_map/co,ct->ot/dot_general | solution.py:61
  118.2 0.1 copy.65
  118.3 23.6 %all_to_all.26 = bf16[8,512,128]{1,2,0:T(8,128)(2,1)S(1)} all-to-all(bf16[8,512,128]{1,2,0:T(8,128)(2,1)S(1)} %bitcast.38), channel_id=1, replica_groups=mesh['ctx'=128,'tp'=8] {'tp'}, dimensions={0} | all-to-all | bytes 2097152 | tf_op jit(solution)/shard_map/all_to_all | solution.py:68
  141.9 0.8 reduce_sum.12
  (17 shorter events, 0.1 us)
Async XLA Ops:
  0.0 72.3 %copy-start.4 = (bf16[512,128,1]{1,0,2:T(8,128)(2,1)S(1)}, bf16[512,128,1]{1,0,2:T(8,128)(2,1)}, u32[]{:S(2)}) copy-start(bf16[512,128,1]{1,0,2:T(8,128)(2,1)} %constant.21) | copy-start | bytes 393220
  1.2 71.6 %copy-start.6 = (f32[256,128]{0,1:T(8,128)S(1)}, f32[256,128]{0,1:T(8,128)}, u32[]{:S(2)}) copy-start(f32[256,128]{0,1:T(8,128)} %constant.15.clone) | copy-start | bytes 393220
  1.2 71.6 %copy-start.7 = (f32[256,128]{0,1:T(8,128)S(1)}, f32[256,128]{0,1:T(8,128)}, u32[]{:S(2)}) copy-start(f32[256,128]{0,1:T(8,128)} %constant.16.clone) | copy-start | bytes 393220
  72.8 0.9 copy-start.1
  74.2 0.9 copy-start.2
  74.2 1.0 copy-start.3
  74.4 0.9 copy-start.9
  75.1 10.2 %copy-start = (bf16[128,512]{1,0:T(8,128)(2,1)S(1)}, bf16[128,512]{1,0:T(8,128)(2,1)}, u32[]{:S(2)}) copy-start(bf16[128,512]{1,0:T(8,128)(2,1)} %param.10) | copy-start | bytes 393220
  75.1 10.3 %copy-start.5 = (bf16[128,512]{1,0:T(8,128)(2,1)S(1)}, bf16[128,512]{1,0:T(8,128)(2,1)}, u32[]{:S(2)}) copy-start(bf16[128,512]{1,0:T(8,128)(2,1)} %param.11) | copy-start | bytes 393220
  75.1 40.0 %copy-start.8 = (f32[512]{0:T(512)S(1)}, f32[512]{0:T(512)}, u32[]{:S(2)}) copy-start(f32[512]{0:T(512)} %param.12) | copy-start | bytes 6148
  76.4 38.7 %all-to-all-start.1 = ((bf16[128,4,128]{2,1,0:T(4,128)(2,1)}), bf16[128,4,128]{2,1,0:T(4,128)(2,1)S(1)}, u32[]{:S(2)}, u32[]{:S(2)}) async-start(bf16[128,4,128]{2,1,0:T(4,128)(2,1)} %copy.53), calls=%async_computation.1 | async-start | bytes 262144 | tf_op jit(solution)/shard_map/all_to_all | solution.py:58

commit v8 on v6

--- a/solution.py
+++ b/solution.py
@@ -56,9 +56,11 @@
     gathered = lax.all_to_all(stack, "ctx", 1, 2, tiled=True)
     conv = long_conv(gathered[0], gathered[1], length).astype(jnp.bfloat16)
     back = lax.all_to_all(conv, "ctx", 1, 0, tiled=True).astype(jnp.float32)
-    source = signal.T.astype(jnp.float32)
-    mixed = (gate.T.astype(jnp.float32) * (back + skip[:, None] * source)).astype(jnp.bfloat16)
-    partial_value = jnp.einsum("co,ct->ot", out_weight, mixed, preferred_element_type=jnp.float32)
+    gating = gate.T.astype(jnp.float32)
+    skipped = (gating * skip[:, None] * signal.T.astype(jnp.float32)).astype(jnp.bfloat16)
+    early = jnp.einsum("co,ct->ot", out_weight, skipped, preferred_element_type=jnp.float32)
+    gated = (gating * back).astype(jnp.bfloat16)
+    partial_value = early + jnp.einsum("co,ct->ot", out_weight, gated, preferred_element_type=jnp.float32)
     return exchange_scatter(partial_value.astype(jnp.bfloat16), "tp").T
 
 

time: 143 us -> 143 us (level)
  waiting for transfers between devices: 29.6 us -> 26.5 us
  matrix products: 4.61 us -> 7.55 us
    all_to_all x1, waiting for transfers between devices: 29.6 us -> 26.5 us  [per_device(): back = lax.all_to_all(conv, 'ctx', 1, 0, tiled=True).astype(jnp.float32)]
    dot_general x1 -> x2, matrix products: 3.03 us -> 5.98 us  [the longest x1 3.03 us: per_device(): jnp.einsum('co,ct->ot', out_weight, skipped, preferred_element_type=jnp.f...]
  transfers between devices with their start and end apart: 1 -> 1, of which waited for: 1 -> 1; matrix products, arithmetic and copies ran while one was open for 0% -> 2% of each run, Pallas kernels for 0% -> 0%
where the time goes in v8:
time: 143 us
  blocking collectives  94.5 us (66%)
  waiting for transfers between devices  26.5 us (19%)
  starting transfers between devices  8.87 us (6%)
  matrix products  7.55 us (5%)
  local copies, waits for them, and re-layouts  2.53 us (2%)
  other arithmetic  2.5 us (2%)
    all_to_all x1, blocking collectives, per_device(): gathered = lax.all_to_all(stack, 'ctx', 1, 2, tiled=True)  70.9 us
    all_to_all x1, waiting for transfers between devices, per_device(): back = lax.all_to_all(conv, 'ctx', 1, 0, tiled=True).astype(jnp.float32)  26.5 us
    all_to_all x1, blocking collectives, exchange_scatter(): lax.all_to_all(value.reshape(count, rows // count, cols), axis, 0, 0, til...  23.6 us
    all_to_all x1, starting transfers between devices, per_device(): back = lax.all_to_all(conv, 'ctx', 1, 0, tiled=True).astype(jnp.float32)  8.87 us
    dot_general x1, matrix products, per_device(): jnp.einsum('co,ct->ot', out_weight, skipped, preferred_element_type=jnp.f...  3.03 us
    dot_general x1, matrix products, per_device(): jnp.einsum('co,ct->ot', out_weight, gated, preferred_element_type=jnp.flo...  2.95 us
  transfers between devices with their start and end apart: 1, of which 1 were waited for; matrix products, arithmetic and copies ran while one was open for 2% of the time, Pallas kernels for 0%

profile of v8, /device:TPU:1, one launch (start us, length us, event | category | flops | bytes accessed | tf_op | source)
XLA Modules:
  0.0 142.7 jit_solution(17530914811149305731)
XLA Ops:
  0.0 1.0 maximum_bitcast_fusion
  1.0 0.2 copy.44
  1.2 70.9 %all_to_all.30 = bf16[2,512,128]{2,0,1:T(2,128)(2,1)S(1)} all-to-all(bf16[2,512,128]{2,0,1:T(2,128)(2,1)S(1)} %copy.44), channel_id=1, replica_groups=mesh['ctx'=128,'tp'=8] {'ctx'}, dimensions={1} | all-to-all | bytes 524288 | tf_op jit(solution)/shard_map/all_to_all | solution.py:56
  72.1 0.2 copy.46
  72.3 0.4 convolution_bitcast_fusion
  72.8 0.3 multiply_subtract_fusion
  73.1 0.6 copy-done.1
  73.7 0.4 fusion.1
  74.2 0.2 multiply_subtract_fusion.1
  74.4 0.4 fusion.7
  74.7 0.3 copy-done.2
  75.1 0.1 copy-done.3
  75.1 0.1 add_convert_fusion
  75.3 0.3 fusion.6
  75.6 0.8 copy.53
  76.4 8.9 %all-to-all-start.1 = ((bf16[4,128,128]{2,0,1:T(4,128)(2,1)}), bf16[4,128,128]{2,0,1:T(4,128)(2,1)S(1)}, u32[]{:S(2)}, u32[]{:S(2)}) async-start(bf16[4,128,128]{2,0,1:T(4,128)(2,1)} %copy.53), calls=%async_computation.1 | async-start | bytes 262144 | tf_op jit(solution)/shard_map/all_to_all | solution.py:58
  85.3 0.1 copy.43
  85.4 0.1 copy.42
  85.6 3.0 %fusion.20 = f32[128,4096]{1,0:T(8,128)S(1)} fusion(bf16[512,4096]{1,0:T(8,128)(2,1)} %param.13, bf16[128,512]{0,1:T(8,128)(2,1)S(1)} %copy.42, bf16[128,512]{0,1:T(8,128)(2,1)S(1)} %copy.43, f32[512]{0:T(512)S(1)} %copy-done.8), kind=kOutput, calls=%fused_computation.33 | convolution fusion | flops 537198592 | bytes 6555648 | tf_op jit(solution)/shard_map/co,ct->ot/dot_general | solution.py:61
  88.6 26.5 %all-to-all-done.1 = bf16[4,128,128]{2,0,1:T(4,128)(2,1)S(1)} async-done(((bf16[4,128,128]{2,0,1:T(4,128)(2,1)}), bf16[4,128,128]{2,0,1:T(4,128)(2,1)S(1)}, u32[]{:S(2)}, u32[]{:S(2)}) %all-to-all-start.1) | async-done | bytes 131104 | tf_op jit(solution)/shard_map/all_to_all | solution.py:58
  115.2 3.0 %fusion = bf16[128,4096]{1,0:T(8,128)(2,1)S(1)} fusion(f32[128,4096]{1,0:T(8,128)S(1)} %fusion.20, bf16[512,4096]{1,0:T(8,128)(2,1)} %param.13, f32[512,128]{1,0:T(8,128)S(1)} %bitcast.50, bf16[128,512]{0,1:T(8,128)(2,1)S(1)} %copy.42), kind=kOutput, calls=%fused_computation.1 | convolution fusion | flops 538116096 | bytes 7733248 | tf_op jit(solution)/shard_map/co,ct->ot/dot_general | solution.py:63
  118.1 0.1 copy.64
  118.2 23.6 %all_to_all.31 = bf16[8,512,128]{1,2,0:T(8,128)(2,1)S(1)} all-to-all(bf16[8,512,128]{1,2,0:T(8,128)(2,1)S(1)} %bitcast.46), channel_id=1, replica_groups=mesh['ctx'=128,'tp'=8] {'tp'}, dimensions={0} | all-to-all | bytes 2097152 | tf_op jit(solution)/shard_map/all_to_all | solution.py:70
  141.9 0.8 reduce_sum.12
  (17 shorter events, 0.1 us)
Async XLA Ops:
  0.0 72.3 %copy-start.4 = (bf16[512,128,1]{1,0,2:T(8,128)(2,1)S(1)}, bf16[512,128,1]{1,0,2:T(8,128)(2,1)}, u32[]{:S(2)}) copy-start(bf16[512,128,1]{1,0,2:T(8,128)(2,1)} %constant.19) | copy-start | bytes 393220
  1.2 71.6 %copy-start.6 = (f32[256,128]{0,1:T(8,128)S(1)}, f32[256,128]{0,1:T(8,128)}, u32[]{:S(2)}) copy-start(f32[256,128]{0,1:T(8,128)} %constant.16.clone) | copy-start | bytes 393220
  1.2 71.6 %copy-start.7 = (f32[256,128]{0,1:T(8,128)S(1)}, f32[256,128]{0,1:T(8,128)}, u32[]{:S(2)}) copy-start(f32[256,128]{0,1:T(8,128)} %constant.15.clone) | copy-start | bytes 393220
  72.8 0.9 copy-start.1
  74.2 0.9 copy-start.2
  74.2 1.0 copy-start.3
  75.1 10.2 %copy-start = (bf16[128,512]{1,0:T(8,128)(2,1)S(1)}, bf16[128,512]{1,0:T(8,128)(2,1)}, u32[]{:S(2)}) copy-start(bf16[128,512]{1,0:T(8,128)(2,1)} %param.9) | copy-start | bytes 393220
  75.1 10.3 %copy-start.5 = (bf16[128,512]{1,0:T(8,128)(2,1)S(1)}, bf16[128,512]{1,0:T(8,128)(2,1)}, u32[]{:S(2)}) copy-start(bf16[128,512]{1,0:T(8,128)(2,1)} %param.10) | copy-start | bytes 393220
  75.1 10.4 %copy-start.8 = (f32[512]{0:T(512)S(1)}, f32[512]{0:T(512)}, u32[]{:S(2)}) copy-start(f32[512]{0:T(512)} %param.11) | copy-start | bytes 6148
  76.4 38.7 %all-to-all-start.1 = ((bf16[4,128,128]{2,0,1:T(4,128)(2,1)}), bf16[4,128,128]{2,0,1:T(4,128)(2,1)S(1)}, u32[]{:S(2)}, u32[]{:S(2)}) async-start(bf16[4,128,128]{2,0,1:T(4,128)(2,1)} %copy.53), calls=%async_computation.1 | async-start | bytes 262144 | tf_op jit(solution)/shard_map/all_to_all | solution.py:58
